TPU v7x, 128 devices: a whole 4x4x4 slice. The times are simulated.
128 devices in a mesh: ctx: 16 (over y, x_lo, core), head: 8 (over x_hi, z).
Axes of the slice: x: 4 (x_hi: 2, x_lo: 2; x = x_hi * 2 + x_lo), y: 4, z: 4, core: 2. Of those that a mesh axis runs over, the one named last changes fastest.
Arguments:
- queries: bfloat16 [4096, 5120], P('ctx', 'head'), may hold values from -6 to 6
- keys: bfloat16 [4096, 5120], P('ctx', 'head'), may hold values from -6 to 6
- values: bfloat16 [4096, 5120], P('ctx', 'head'), may hold values from -16 to 16
- out_weight: bfloat16 [5120, 5120], P('head'), may hold values from -0.078125 to 0.078125
- cotangent: bfloat16 [4096, 5120], P('ctx', 'head'), may hold values from -16 to 16
- contacts: int32 [32, 32], replicated, may hold values 0 or 1
- chains: int32 [32], replicated, may hold values from 0 to 3, never falling along the last dimension, each value on 1 to 16 neighbouring positions
Outputs:
- mixed: bfloat16 [4096, 5120], P('ctx', 'head')
- query_grad: bfloat16 [4096, 5120], P('ctx', 'head')
- key_grad: bfloat16 [4096, 5120], P('ctx', 'head')
- value_grad: bfloat16 [4096, 5120], P('ctx', 'head')
Inputs may be any that keep to these rules, and one draw needn't show every extreme that they name: `chains`: chain numbers never fall along the blocks; each chain has 1 to 16 blocks, one exactly 16.
All inputs are finite; a program needn't handle non-finite values.
Results may differ from a plain program's by a relative error of at most 0.02.
Values may be sent and summed in bfloat16 or wider, within the bound.
No kernel may reach another device: no remote copies, remote signals or barrier semaphores. Data moves between devices by JAX's collectives and lax.ppermute only.
A program may use at most 192 MiB of HBM per device.

v0:
```python
import jax
import jax.numpy as jnp
from jax import lax
from jax.sharding import PartitionSpec as P

HEAD_SIZE = 128
BLOCK = 128


NEG = -1e30


def rounded(value):
    return lax.optimization_barrier(value.astype(jnp.bfloat16)).astype(jnp.float32)


def block_mask(allowed, row_start, col_start, row_count, col_count):
    part_mask = lax.dynamic_slice(
        allowed, (row_start // BLOCK, col_start // BLOCK), (row_count // BLOCK, col_count // BLOCK)
    )
    part_mask = jnp.repeat(jnp.repeat(part_mask, BLOCK, axis=0), BLOCK, axis=1)
    return part_mask[:, None, :]


def forward_fold(q_three, allowed, own_start):
    scale = HEAD_SIZE ** (-0.5)
    rows, heads, size = q_three.shape

    def step(carry, piece, start):
        best, total, accum = carry
        key_rows, value_rows = piece
        count = key_rows.shape[0]
        k_three = key_rows.reshape(count, heads, size)
        v_three = value_rows.reshape(count, heads, size)
        scores = (
            jnp.einsum("qhd,khd->qhk", q_three, k_three, preferred_element_type=jnp.float32) * scale
        )
        keep = block_mask(allowed, own_start, start, rows, count)
        scores = jnp.where(keep, scores, NEG)
        best_new = jnp.maximum(best, jnp.max(scores, axis=2))
        weights = jnp.where(keep, jnp.exp(scores - best_new[:, :, None]), 0.0)
        total = jnp.sum(weights, axis=2)
        accum = jnp.einsum(
            "qhk,khd->qhd",
            weights.astype(jnp.bfloat16),
            v_three,
            preferred_element_type=jnp.float32,
        )
        return (best_new, total, accum)

    return step


def key_fold(q_three, g_three, lse, delta, allowed, own_start):
    scale = HEAD_SIZE ** (-0.5)
    rows, heads, size = q_three.shape

    def step(carry, piece, start):
        key_rows, value_rows = piece
        count = key_rows.shape[0]
        groups = count // rows
        k_three = key_rows.reshape(count, heads, size)
        v_three = value_rows.reshape(count, heads, size)
        scores = (
            jnp.einsum("qhd,khd->qhk", q_three, k_three, preferred_element_type=jnp.float32) * scale
        )
        keep = block_mask(allowed, own_start, start, rows, count)
        probs = jnp.where(keep, jnp.exp(scores - lse[:, :, None]), 0.0)
        dprob = jnp.einsum("qhd,khd->qhk", g_three, v_three, preferred_element_type=jnp.float32)
        dscore = (probs * (dprob - delta[:, :, None])).astype(jnp.bfloat16)
        q_parts = (
            jnp.einsum(
                "qhgk,gkhd->gqhd",
                dscore.reshape(rows, heads, groups, rows),
                k_three.reshape(groups, rows, heads, size),
                preferred_element_type=jnp.float32,
            )
            * scale
        )
        q_accum = jnp.sum(rounded(q_parts), axis=0)
        key_part = (
            jnp.einsum("qhk,qhd->khd", dscore, q_three, preferred_element_type=jnp.float32) * scale
        ).astype(jnp.bfloat16)
        value_part = jnp.einsum(
            "qhk,qhd->khd", probs.astype(jnp.bfloat16), g_three, preferred_element_type=jnp.float32
        ).astype(jnp.bfloat16)
        key_term = key_part.reshape(count, heads * size)
        value_term = value_part.reshape(count, heads * size)
        return (q_accum, key_term, value_term)

    return step


def per_device(queries, keys, values, out_weight, cotangent, contacts, chains):
    rows = queries.shape[0]
    size = HEAD_SIZE
    heads = queries.shape[1] // size
    width = heads * size
    length = rows * lax.axis_size("ctx")
    allowed = jnp.logical_or(chains[:, None] == chains[None, :], contacts > 0)
    own_start = lax.axis_index("ctx") * rows
    q_three = queries.reshape(rows, heads, size)
    init = (
        jnp.full((rows, heads), NEG, jnp.float32),
        jnp.zeros((rows, heads), jnp.float32),
        jnp.zeros((rows, heads, size), jnp.float32),
    )
    forward_step = forward_fold(q_three, allowed, own_start)
    best, total, accum = forward_step(
        init,
        (
            lax.all_gather(keys, "ctx", axis=0, tiled=True),
            lax.all_gather(values, "ctx", axis=0, tiled=True),
        ),
        jnp.int32(0),
    )
    attended = (accum / total[:, :, None]).astype(jnp.bfloat16)
    lse = best + jnp.log(total)
    projected = jnp.dot(
        attended.reshape(rows, width), out_weight, preferred_element_type=jnp.float32
    )
    mixed = lax.psum_scatter(
        projected.astype(jnp.bfloat16), "head", scatter_dimension=1, tiled=True
    )
    full_cotangent = lax.all_gather(cotangent, "head", axis=1, tiled=True)
    grads = lax.dot_general(
        full_cotangent, out_weight, (((1,), (1,)), ((), ())), preferred_element_type=jnp.float32
    ).astype(jnp.bfloat16)
    g_three = grads.reshape(rows, heads, size)
    delta = jnp.sum(g_three.astype(jnp.float32) * attended.astype(jnp.float32), axis=2)
    start_carry = (
        jnp.zeros((rows, heads, size), jnp.float32),
        jnp.zeros((length, width), jnp.bfloat16),
        jnp.zeros((length, width), jnp.bfloat16),
    )
    step = key_fold(q_three, g_three, lse, delta, allowed, own_start)
    q_accum, key_term, value_term = step(
        start_carry,
        (
            lax.all_gather(keys, "ctx", axis=0, tiled=True),
            lax.all_gather(values, "ctx", axis=0, tiled=True),
        ),
        jnp.int32(0),
    )
    key_sum, value_sum = (
        lax.psum_scatter(
            key_term.astype(jnp.float32).astype(jnp.bfloat16),
            "ctx",
            scatter_dimension=0,
            tiled=True,
        ).astype(jnp.float32),
        lax.psum_scatter(
            value_term.astype(jnp.float32).astype(jnp.bfloat16),
            "ctx",
            scatter_dimension=0,
            tiled=True,
        ).astype(jnp.float32),
    )
    query_grad = q_accum.reshape(rows, width).astype(jnp.bfloat16)
    key_grad = key_sum.astype(jnp.bfloat16)
    value_grad = value_sum.astype(jnp.bfloat16)
    return (mixed, query_grad, key_grad, value_grad)


def solution(mesh):
    in_specs = (
        P("ctx", "head"),
        P("ctx", "head"),
        P("ctx", "head"),
        P("head", None),
        P("ctx", "head"),
        P(),
        P(),
    )
    out_specs = (P("ctx", "head"), P("ctx", "head"), P("ctx", "head"), P("ctx", "head"))
    return jax.shard_map(
        per_device, mesh=mesh, in_specs=in_specs, out_specs=out_specs, check_vma=False
    )
```

profile of v0, /device:TPU:0, one launch (start us, length us, event | category | flops | bytes accessed | tf_op | source)
XLA Modules:
  0.0 425.8 jit_solution(9775837126205943707)
XLA Ops:
  7.9 1.9 copy.44
  12.4 1.1 copy.45
  13.5 57.3 %all-gather.8.cloned.1.call-done = bf16[256,5120]{1,0:T(8,128)(2,1)} async-done(((bf16[256,640]{1,0:T(8,128)(2,1)}), bf16[256,5120]{1,0:T(8,128)(2,1)}) %all-gather.8.cloned.1.call-update) | async-done | bytes 2621456 | tf_op jit(solution)/shard_map/all_gather | solution.py:125
  70.8 5.9 %convolution_convert_fusion.1 = bf16[256,640]{1,0:T(8,128)(2,1)S(1)} fusion(bf16[256,5120]{1,0:T(8,128)(2,1)} %all-gather.8.cloned.1.call-done, bf16[640,5120]{1,0:T(8,128)(2,1)} %param.10), kind=kOutput, calls=%fused_computation.28 | convolution fusion | flops 1677885440 | bytes 9502720 | tf_op jit(solution)/shard_map/dot_general | solution.py:126
  76.9 43.3 %all-gather.4.cloned.1.call-done = bf16[4096,640]{0,1:T(8,128)(2,1)} async-done(((bf16[256,640]{0,1:T(8,128)(2,1)}), bf16[4096,640]{0,1:T(8,128)(2,1)}) %all-gather.4.cloned.1.call-update) | async-done | bytes 5242896 | tf_op jit(solution)/shard_map/all_gather | solution.py:112
  120.5 12.9 %fusion.4 = (f32[256,5]{0,1:T(8,128)S(1)}, f32[5,4096,256]{2,1,0:T(8,128)}) fusion(pred[256,4096]{0,1:T(8,128)(4,1)S(1)} %bitcast.89, bf16[4096,5,128]{0,2,1:T(8,128)(2,1)} %bitcast.85, bf16[256,5,128]{0,2,1:T(8,128)(2,1)S(1)} %bitcast.98), kind=kOutput, calls=%fused_computation.8 | convolution fusion | flops 1357904640 | bytes 27595776 | tf_op jit(solution)/shard_map/qhd,khd->qhk/dot_general | solution.py:36
  133.3 10.0 %fusion.6 = f32[256,5]{0,1:T(8,128)S(1)} fusion(f32[5,4096,256]{2,1,0:T(8,128)} %get-tuple-element.13, f32[256,5]{0,1:T(8,128)S(1)} %broadcast_maximum_fusion, pred[256,4096]{0,1:T(8,128)(4,1)S(1)} %bitcast.90), kind=kLoop, calls=%fused_computation.10 | loop fusion | flops 26213120 | bytes 22030336 | tf_op jit(solution)/shard_map/reduce_sum | solution.py:42
  143.4 17.5 %all-gather.6.cloned.1.call-done = bf16[4096,640]{1,0:T(8,128)(2,1)} async-done(((bf16[256,640]{1,0:T(8,128)(2,1)}), bf16[4096,640]{1,0:T(8,128)(2,1)}) %all-gather.6.cloned.1.call-update) | async-done | bytes 5242896 | tf_op jit(solution)/shard_map/all_gather | solution.py:113
  160.9 7.9 %copy.48 = bf16[4096,640]{0,1:T(8,128)(2,1)} copy(bf16[4096,640]{1,0:T(8,128)(2,1)} %all-gather.6.cloned.1.call-done) | data formatting | bytes 10485760 | tf_op jit(solution)/shard_map/all_gather | solution.py:113
  168.8 13.2 %multiply_reduce_fusion = (f32[256,5]{0,1:T(8,128)S(1)}, bf16[256,5,128]{0,2,1:T(8,128)(2,1)S(1)}) fusion(bf16[256,5,128]{0,2,1:T(8,128)(2,1)S(1)} %bitcast.103, f32[256,5]{0,1:T(8,128)S(1)} %fusion.6, bf16[4096,5,128]{0,2,1:T(8,128)(2,1)} %bitcast.94, f32[5,4096,256]{2,1,0:T(8,128)} %get-tuple-element.13, f32[256,5]{0,1:T(8,128)S(1)} %broadcast_maximum_fusion, ...), kind=kOutput, calls=%fused_computation.31 | convolution fusion | flops 1369373440 | bytes 27933696 | tf_op jit(solution)/shard_map/qhk,khd->qhd/dot_general | solution.py:43
  182.0 5.1 %convolution_convert_fusion = bf16[256,5120]{1,0:T(8,128)(2,1)S(1)} fusion(bf16[256,640]{0,1:T(8,128)(2,1)S(1)} %bitcast.101, bf16[640,5120]{1,0:T(8,128)(2,1)} %param.10), kind=kOutput, calls=%fused_computation.23 | convolution fusion | flops 1679032320 | bytes 9502720 | tf_op jit(solution)/shard_map/dot_general | solution.py:119
  187.1 2.6 copy.72
  189.8 11.1 %fusion.19 = bf16[5,128,4096]{2,1,0:T(8,128)(2,1)} fusion(bf16[256,5,128]{0,2,1:T(8,128)(2,1)S(1)} %bitcast.104, f32[5,4096,256]{2,1,0:T(8,128)} %get-tuple-element.13, f32[256,5]{0,1:T(8,128)S(1)} %log_add_fusion, pred[256,4096]{0,1:T(8,128)(4,1)} %bitcast.92), kind=kOutput, calls=%fused_computation.24 | convolution fusion | flops 1365770240 | bytes 27595776 | tf_op jit(solution)/shard_map/qhk,qhd->khd/dot_general | solution.py:84
  200.9 7.9 %copy.60 = bf16[4096,640]{1,0:T(8,128)(2,1)} copy(bf16[4096,640]{0,1:T(8,128)(2,1)} %bitcast.97) | data formatting | bytes 10485760 | tf_op jit(solution)/shard_map/reshape | solution.py:88
  209.0 16.8 %fusion.1 = bf16[256,5,4096]{0,2,1:T(8,128)(2,1)} fusion(f32[5,4096,256]{2,1,0:T(8,128)} %get-tuple-element.13, f32[256,5]{0,1:T(8,128)S(1)} %get-tuple-element.14, f32[256,5]{0,1:T(8,128)S(1)} %log_add_fusion, pred[256,4096]{0,1:T(8,128)(4,1)S(1)} %bitcast.93, bf16[256,5,128]{0,2,1:T(8,128)(2,1)S(1)} %bitcast.105, bf16[4096,5,128]{0,2,1:T(8,128)(2,1)} %bitcast.95), kind=kOutput, calls=%fused_computation.2 | convolution fusion | flops 1373634560 | bytes 38086656 | tf_op jit(solution)/shard_map/qhd,khd->qhk/dot_general | solution.py:69
  225.7 10.1 %multiply_convert_fusion = bf16[5,4096,128]{1,2,0:T(8,128)(2,1)} fusion(bf16[256,5,4096]{0,2,1:T(8,128)(2,1)} %fusion.1, bf16[256,5,128]{0,2,1:T(8,128)(2,1)S(1)} %bitcast.99), kind=kOutput, calls=%fused_computation.15 | convolution fusion | flops 1347420160 | bytes 16056320 | tf_op jit(solution)/shard_map/qhk,qhd->khd/dot_general | solution.py:82
  235.8 7.9 %copy.58 = bf16[4096,640]{1,0:T(8,128)(2,1)} copy(bf16[4096,640]{0,1:T(8,128)(2,1)} %bitcast.84) | data formatting | bytes 10485760 | tf_op jit(solution)/shard_map/reshape | solution.py:87
  243.7 4.3 %copy.75 = bf16[80,8,16,256]{3,2,1,0:T(8,128)(2,1)S(1)} copy(bf16[80,8,16,256]{3,1,2,0:T(8,128)(2,1)} %bitcast.86) | data formatting | bytes 10485760
  248.0 9.5 %fusion.22 = bf16[16,256,5,128]{3,1,2,0:T(8,128)(2,1)} fusion(bf16[16,256,5,128]{1,0,3,2:T(8,128)(2,1)S(1)} %bitcast.96, bf16[256,5,16,256]{0,3,2,1:T(8,128)(2,1)} %bitcast.88), kind=kOutput, calls=%fused_computation.25 | convolution fusion | flops 1347420160 | bytes 20971520 | tf_op jit(solution)/shard_map/qhgk,gkhd->gqhd/dot_general | solution.py:72
  257.5 3.6 reduce_sum.32
  262.2 6.6 %reduce-scatter.10.cloned.1.call-done = bf16[640,256]{1,0:T(8,128)(2,1)} async-done(((bf16[5120,256]{1,0:T(8,128)(2,1)}), bf16[640,256]{1,0:T(8,128)(2,1)}) %reduce-scatter.10.cloned.1.call-update) | async-done | bytes 327696
  268.7 1.9 copy.73
  270.6 73.0 %reduce-scatter.8.cloned.1.call-done = bf16[256,640]{1,0:T(8,128)(2,1)} async-done(((bf16[4096,640]{1,0:T(8,128)(2,1)}), bf16[256,640]{1,0:T(8,128)(2,1)}) %reduce-scatter.8.cloned.1.call-update) | async-done | bytes 327696 | tf_op jit(solution)/shard_map/reduce_scatter | solution.py:152
  343.6 75.4 %reduce-scatter.6.cloned.1.call-done = bf16[256,640]{1,0:T(8,128)(2,1)} async-done(((bf16[4096,640]{1,0:T(8,128)(2,1)}), bf16[256,640]{1,0:T(8,128)(2,1)}) %reduce-scatter.6.cloned.1.call-update) | async-done | bytes 327696 | tf_op jit(solution)/shard_map/reduce_scatter | solution.py:146
  (27 shorter events, 4.9 us)
Async XLA Ops:
  7.2 63.6 %all-gather.8.cloned.1.call-start = ((), (), s32[]{:S(2)}) async-start(), calls=%async_computation.5 | async-start | bytes 2949120 | tf_op jit(solution)/shard_map/all_gather | solution.py:125
  7.9 112.3 %all-gather.4.cloned.1.call-start = ((), (), s32[]{:S(2)}) async-start(), calls=%async_computation.3 | async-start | bytes 5570560 | tf_op jit(solution)/shard_map/all_gather | solution.py:112
  9.8 151.1 %all-gather.6.cloned.1.call-start = ((), (), s32[]{:S(2)}) async-start(), calls=%async_computation.4 | async-start | bytes 5570560 | tf_op jit(solution)/shard_map/all_gather | solution.py:113
  10.6 258.2 %reduce-scatter.10.cloned.1.call-start = ((), (), s32[]{:S(2)}) async-start(), calls=%async_computation.8 | async-start | bytes 2949120
  120.5 48.4 %copy-start = (pred[256,32,128]{0,2,1:T(8,128)(4,1)}, pred[256,32,128]{0,2,1:T(8,128)(4,1)S(1)}, u32[]{:S(2)}) copy-start(pred[256,32,128]{0,2,1:T(8,128)(4,1)S(1)} %broadcast_in_dim.42) | copy-start | bytes 3145732
  189.7 153.9 %reduce-scatter.8.cloned.1.call-start = ((), (), s32[]{:S(2)}) async-start(), calls=%async_computation.7 | async-start | bytes 5570560 | tf_op jit(solution)/shard_map/reduce_scatter | solution.py:152
  200.9 8.0 %copy-start.1 = (pred[256,32,128]{0,2,1:T(8,128)(4,1)S(1)}, pred[256,32,128]{0,2,1:T(8,128)(4,1)}, u32[]{:S(2)}) copy-start(pred[256,32,128]{0,2,1:T(8,128)(4,1)} %copy-done) | copy-start | bytes 3145732
  208.9 210.1 %reduce-scatter.6.cloned.1.call-start = ((), (), s32[]{:S(2)}) async-start(), calls=%async_computation.6 | async-start | bytes 5570560 | tf_op jit(solution)/shard_map/reduce_scatter | solution.py:146
Sparse Core Ops, SparseCore 0:
  10.4 60.3 all-gather.7
  73.0 47.1 all-gather.3
  121.9 38.9 all-gather.5
  189.9 78.8 reduce-scatter.9
  271.6 71.9 reduce-scatter.7
  346.4 72.5 reduce-scatter.5
where the time goes:
time: 427 us; the launch traced here: 426 us
  waiting for transfers between devices  275 us (64%)
  matrix products  84.5 us (20%)
  local copies, waits for them, and re-layouts  38 us (9%)
  other arithmetic  14.4 us (3%)
  between operations  14.2 us (3%)
    reduce_scatter x1, waiting for transfers between devices, per_device(): lax.psum_scatter(key_term.astype(jnp.float32).astype(jnp.bfloat16), 'ctx'...  75.4 us
    reduce_scatter x1, waiting for transfers between devices, per_device(): lax.psum_scatter(value_term.astype(jnp.float32).astype(jnp.bfloat16), 'ct...  73 us
    all_gather x1, waiting for transfers between devices, per_device(): full_cotangent = lax.all_gather(cotangent, 'head', axis=1, tiled=True)  57.3 us
    all_gather x1, waiting for transfers between devices, per_device(): lax.all_gather(keys, 'ctx', axis=0, tiled=True)  43.3 us
    all_gather x1, waiting for transfers between devices, per_device(): lax.all_gather(values, 'ctx', axis=0, tiled=True)  17.5 us
    dot_general x1, matrix products, step(): jnp.einsum('qhd,khd->qhk', g_three, v_three, preferred_element_type=jnp.f...  16.8 us
    dot_general x1, matrix products, step(): jnp.einsum('qhk,khd->qhd', weights.astype(jnp.bfloat16), v_three, preferr...  13.2 us
    dot_general x1, matrix products, step(): jnp.einsum('qhd,khd->qhk', q_three, k_three, preferred_element_type=jnp.f...  12.9 us
  transfers between devices with their start and end apart: 6, of which 6 were waited for; matrix products, arithmetic and copies ran while one was open for 25% of the time, Pallas kernels for 0%

commit v1 on v0

v1 whole, which is shorter than its diff:
```python
import jax
import jax.numpy as jnp
from jax import lax
from jax.sharding import Mesh
from jax.sharding import PartitionSpec as P

HEAD_SIZE = 128
BLOCK = 128

NEG = -1e30
CTX = ("ctxo", "core")
SWAP = [(0, 1), (1, 0)]


def swap(value):
    return lax.ppermute(value, "core", SWAP)


def pair_rows(own, other, core):
    first = jnp.where(core == 0, own, other)
    second = jnp.where(core == 0, other, own)
    return jnp.concatenate([first, second], axis=0)


def halves(value, core):
    rows = value.shape[0] // 2
    top, bottom = value[:rows], value[rows:]
    own = jnp.where(core == 0, top, bottom)
    other = jnp.where(core == 0, bottom, top)
    return own, other


def per_device(queries, keys, values, out_weight, cotangent, contacts, chains):
    scale = HEAD_SIZE ** (-0.5)
    rows = queries.shape[0]
    size = HEAD_SIZE
    heads = queries.shape[1] // size
    width = heads * size
    n_out = lax.axis_size("ctxo")
    n_head = lax.axis_size("head")
    core = lax.axis_index("core")
    outer = lax.axis_index("ctxo")
    allowed = jnp.logical_or(chains[:, None] == chains[None, :], contacts > 0)
    q_blocks = rows // BLOCK

    spread = jnp.broadcast_to(cotangent[:, None, :], (rows, n_head, width))
    full_cotangent = lax.all_to_all(spread, "head", 1, 1, tiled=True).reshape(rows, n_head * width)
    grads = lax.dot_general(
        full_cotangent, out_weight, (((1,), (1,)), ((), ())), preferred_element_type=jnp.float32
    ).astype(jnp.bfloat16)

    key_half = lax.all_gather(keys, "ctxo", axis=0, tiled=True)
    value_half = lax.all_gather(values, "ctxo", axis=0, tiled=True)
    count = key_half.shape[0]

    q_chip = pair_rows(queries, swap(queries), core)
    chip_rows = 2 * rows
    q_three = q_chip.reshape(chip_rows, heads, size)
    k_three = key_half.reshape(count, heads, size)
    v_three = value_half.reshape(count, heads, size)

    row_blocks = outer * (2 * q_blocks) + jnp.arange(2 * q_blocks)
    shard = 2 * jnp.arange(n_out) + core
    col_blocks = (shard[:, None] * q_blocks + jnp.arange(q_blocks)[None, :]).reshape(-1)
    part_mask = allowed[row_blocks][:, col_blocks]
    keep = jnp.repeat(jnp.repeat(part_mask, BLOCK, axis=0), BLOCK, axis=1)[:, None, :]

    scores = jnp.einsum("qhd,khd->qhk", q_three, k_three, preferred_element_type=jnp.float32) * scale
    scores = jnp.where(keep, scores, NEG)
    best = jnp.max(scores, axis=2)
    weights = jnp.where(keep, jnp.exp(scores - best[:, :, None]), 0.0)
    total = jnp.sum(weights, axis=2)
    accum = jnp.einsum(
        "qhk,khd->qhd", weights.astype(jnp.bfloat16), v_three, preferred_element_type=jnp.float32
    )

    state = jnp.concatenate([best, total, accum.reshape(chip_rows, width)], axis=1)
    own_state, other_state = halves(state, core)
    got_state = swap(other_state)
    best_a, total_a, acc_a = own_state[:, :heads], own_state[:, heads:2 * heads], own_state[:, 2 * heads:]
    best_b, total_b, acc_b = got_state[:, :heads], got_state[:, heads:2 * heads], got_state[:, 2 * heads:]
    best_m = jnp.maximum(best_a, best_b)
    fa = jnp.exp(best_a - best_m)
    fb = jnp.exp(best_b - best_m)
    total_m = total_a * fa + total_b * fb
    acc_m = acc_a.reshape(rows, heads, size) * fa[:, :, None] + acc_b.reshape(rows, heads, size) * fb[:, :, None]
    attended = (acc_m / total_m[:, :, None]).astype(jnp.bfloat16)
    lse = best_m + jnp.log(total_m)

    projected = jnp.dot(attended.reshape(rows, width), out_weight, preferred_element_type=jnp.float32)
    parts = lax.all_to_all(
        projected.astype(jnp.bfloat16).reshape(rows, n_head, width), "head", 1, 1, tiled=True
    )
    mixed = jnp.sum(parts.astype(jnp.float32), axis=1).astype(jnp.bfloat16)

    g_own = grads.reshape(rows, heads, size)
    delta = jnp.sum(g_own.astype(jnp.float32) * attended.astype(jnp.float32), axis=2)
    side = jnp.concatenate([lse, delta], axis=1)
    side_chip = pair_rows(side, swap(side), core)
    lse_chip, delta_chip = side_chip[:, :heads], side_chip[:, heads:]
    g_chip = pair_rows(grads, swap(grads), core).reshape(chip_rows, heads, size)

    scores = jnp.einsum("qhd,khd->qhk", q_three, k_three, preferred_element_type=jnp.float32) * scale
    probs = jnp.where(keep, jnp.exp(scores - lse_chip[:, :, None]), 0.0)
    dprob = jnp.einsum("qhd,khd->qhk", g_chip, v_three, preferred_element_type=jnp.float32)
    dscore = (probs * (dprob - delta_chip[:, :, None])).astype(jnp.bfloat16)

    q_part = jnp.einsum("qhk,khd->qhd", dscore, k_three, preferred_element_type=jnp.float32) * scale
    q_own, q_other = halves(q_part.reshape(chip_rows, width), core)
    query_grad = (q_own + swap(q_other)).astype(jnp.bfloat16)

    key_part = (
        jnp.einsum("qhk,qhd->khd", dscore, q_three, preferred_element_type=jnp.float32) * scale
    ).astype(jnp.bfloat16)
    value_part = jnp.einsum(
        "qhk,qhd->khd", probs.astype(jnp.bfloat16), g_chip, preferred_element_type=jnp.float32
    ).astype(jnp.bfloat16)
    key_grad = lax.psum_scatter(key_part.reshape(count, width), "ctxo", scatter_dimension=0, tiled=True)
    value_grad = lax.psum_scatter(value_part.reshape(count, width), "ctxo", scatter_dimension=0, tiled=True)
    return (mixed, query_grad, key_grad, value_grad)


def solution(mesh):
    devices = mesh.devices
    n_ctx, n_head = devices.shape
    split = Mesh(devices.reshape(n_ctx // 2, 2, n_head), ("ctxo", "core", "head"))
    rows_spec = P(CTX, "head")
    in_specs = (rows_spec, rows_spec, rows_spec, P("head", None), rows_spec, P(), P())
    out_specs = (rows_spec, rows_spec, rows_spec, rows_spec)
    return jax.shard_map(
        per_device, mesh=split, in_specs=in_specs, out_specs=out_specs, check_vma=False
    )
```

time: 427 us -> 381 us (0.89)
  waiting for transfers between devices: 275 us -> 224 us
  starting transfers between devices: 0.24 us -> 16 us
  matrix products: 84.5 us -> 69.9 us
    all_to_all x0 -> x2, waiting for transfers between devices: none -> 96.6 us  [the longest x1 52.2 us: per_device(): lax.all_to_all(spread, 'head', 1, 1, tiled=True)]
    reduce_scatter x2, waiting for transfers between devices: 148 us -> 64.5 us  [the longest x1 64.5 us: per_device(): lax.psum_scatter(value_part.reshape(count, width), 'ctxo', scatter_dimens...]
    all_gather x3 -> x2, waiting for transfers between devices: 118 us -> 59.9 us  [the longest x1 45.7 us: per_device(): value_half = lax.all_gather(values, 'ctxo', axis=0, tiled=True)]
    all_to_all x0 -> x2, starting transfers between devices: none -> 14.4 us  [the longest x1 7.89 us: per_device(): lax.all_to_all(spread, 'head', 1, 1, tiled=True)]
    dot_general x6, matrix products: 73.6 us -> 59.6 us  [the longest x1 15.5 us: per_device(): jnp.einsum('qhd,khd->qhk', g_chip, v_three, preferred_element_type=jnp.fl...]
    unnamed x7 -> x4, waiting for transfers between devices: 8 us -> 0.74 us
    broadcast_in_dim x2 -> x3, local copies, waits for them, and re-layouts: 0.37 us -> 6.21 us  [the longest x1 3.47 us: per_device(): jnp.repeat(jnp.repeat(part_mask, BLOCK, axis=0), BLOCK, axis=1)[:, None, :]]
    reduce_sum x2 -> x3, other arithmetic: 13.6 us -> 8.02 us  [the longest x1 6.71 us: per_device(): total = jnp.sum(weights, axis=2)]
  transfers between devices with their start and end apart: 6 -> 11, of which waited for: 6 -> 8; matrix products, arithmetic and copies ran while one was open for 25% -> 18% of each run, Pallas kernels for 0% -> 0%
where the time goes in v1:
time: 381 us; the launch traced here: 380 us
  waiting for transfers between devices  224 us (59%)
  matrix products  69.9 us (18%)
  local copies, waits for them, and re-layouts  40.7 us (11%)
  starting transfers between devices  16 us (4%)
  other arithmetic  14.6 us (4%)
  between operations  14 us (4%)
    reduce_scatter x1, waiting for transfers between devices, per_device(): lax.psum_scatter(value_part.reshape(count, width), 'ctxo', scatter_dimens...  64.5 us
    all_to_all x1, waiting for transfers between devices, per_device(): lax.all_to_all(spread, 'head', 1, 1, tiled=True)  52.2 us
    all_gather x1, waiting for transfers between devices, per_device(): value_half = lax.all_gather(values, 'ctxo', axis=0, tiled=True)  45.7 us
    all_to_all x1, waiting for transfers between devices, per_device(): lax.all_to_all(projected.astype(jnp.bfloat16).reshape(rows, n_head, width...  44.3 us
    dot_general x1, matrix products, per_device(): jnp.einsum('qhd,khd->qhk', g_chip, v_three, preferred_element_type=jnp.fl...  15.5 us
    all_gather x1, waiting for transfers between devices, per_device(): key_half = lax.all_gather(keys, 'ctxo', axis=0, tiled=True)  14.2 us
    dot_general x1, matrix products, per_device(): jnp.einsum('qhk,qhd->khd', probs.astype(jnp.bfloat16), g_chip, preferred_...  11.4 us
    dot_general x1, matrix products, per_device(): jnp.einsum('qhk,khd->qhd', weights.astype(jnp.bfloat16), v_three, preferr...  11.1 us
  transfers between devices with their start and end apart: 11, of which 8 were waited for; matrix products, arithmetic and copies ran while one was open for 18% of the time, Pallas kernels for 0%

profile of v1, /device:TPU:0, one launch (start us, length us, event | category | flops | bytes accessed | tf_op | source)
XLA Modules:
  0.0 379.6 jit_solution(15274366431642683863)
XLA Ops:
  7.2 1.9 copy.65
  9.2 2.7 broadcast_in_dim.54
  11.9 7.9 %all-to-all-start.1 = ((bf16[256,8,640]{2,0,1:T(8,128)(2,1)}), bf16[256,8,640]{2,0,1:T(8,128)(2,1)}, u32[]{:S(2)}, u32[]{:S(2)}) async-start(bf16[256,8,640]{2,0,1:T(8,128)(2,1)} %broadcast_in_dim.54), calls=%async_computation.1 | async-start | bytes 5242880 | tf_op jit(solution)/shard_map/all_to_all | solution.py:47
  22.4 3.5 broadcast_in_dim.49
  27.8 52.2 %all-to-all-done.1 = bf16[256,8,640]{2,0,1:T(8,128)(2,1)} async-done(((bf16[256,8,640]{2,0,1:T(8,128)(2,1)}), bf16[256,8,640]{2,0,1:T(8,128)(2,1)}, u32[]{:S(2)}, u32[]{:S(2)}) %all-to-all-start.1) | async-done | bytes 2621472 | tf_op jit(solution)/shard_map/all_to_all | solution.py:47
  80.1 4.4 %copy.70 = bf16[256,8,640]{0,2,1:T(8,128)(2,1)} copy(bf16[256,8,640]{2,0,1:T(8,128)(2,1)} %all-to-all-done.1) | data formatting | bytes 5242880 | tf_op jit(solution)/shard_map/all_to_all | solution.py:47
  84.5 14.2 %all-gather.3.cloned.1.call-done = bf16[2048,640]{0,1:T(8,128)(2,1)} async-done(((bf16[256,640]{0,1:T(8,128)(2,1)}), bf16[2048,640]{0,1:T(8,128)(2,1)}) %all-gather.3.cloned.1.call-update) | async-done | bytes 2621456 | tf_op jit(solution)/shard_map/all_gather | solution.py:52
  98.7 6.1 %fusion.4 = (f32[512,5]{0,1:T(8,128)S(1)}, f32[5,512,2048]{2,1,0:T(8,128)S(1)}) fusion(pred[512,2048]{1,0:T(8,128)(4,1)S(1)} %bitcast.92, bf16[512,5,128]{0,2,1:T(8,128)(2,1)} %bitcast.100, bf16[2048,5,128]{0,2,1:T(8,128)(2,1)} %bitcast.102), kind=kOutput, calls=%fused_computation.10 | convolution fusion | flops 1357903360 | bytes 25307136 | tf_op jit(solution)/shard_map/qhd,khd->qhk/dot_general | solution.py:68
  104.8 7.0 %copy-done = f32[5,512,2048]{2,1,0:T(8,128)} copy-done((f32[5,512,2048]{2,1,0:T(8,128)}, f32[5,512,2048]{2,1,0:T(8,128)S(1)}, u32[]{:S(2)}) %copy-start) | copy-done | bytes 20971544
  111.8 6.7 %fusion.7 = f32[512,5]{0,1:T(8,128)S(1)} fusion(f32[5,512,2048]{2,1,0:T(8,128)S(1)} %get-tuple-element.24, f32[512,5]{0,1:T(8,128)S(1)} %get-tuple-element.23, pred[512,2048]{1,0:T(8,128)(4,1)S(1)} %bitcast.93), kind=kLoop, calls=%fused_computation.13 | loop fusion | flops 26211840 | bytes 22040576 | tf_op jit(solution)/shard_map/reduce_sum | solution.py:72
  118.6 45.7 %all-gather.5.cloned.1.call-done = bf16[2048,640]{1,0:T(8,128)(2,1)} async-done(((bf16[256,640]{1,0:T(8,128)(2,1)}), bf16[2048,640]{1,0:T(8,128)(2,1)}) %all-gather.5.cloned.1.call-update) | async-done | bytes 2621456 | tf_op jit(solution)/shard_map/all_gather | solution.py:53
  164.3 4.5 %copy.68 = bf16[2048,640]{0,1:T(8,128)(2,1)} copy(bf16[2048,640]{1,0:T(8,128)(2,1)} %all-gather.5.cloned.1.call-done) | data formatting | bytes 5242880 | tf_op jit(solution)/shard_map/all_gather | solution.py:53
  168.8 11.1 %fusion.10 = f32[5,512,128]{1,2,0:T(8,128)S(1)} fusion(bf16[2048,5,128]{0,2,1:T(8,128)(2,1)} %bitcast.105, f32[5,512,2048]{2,1,0:T(8,128)} %copy-done, f32[512,5]{0,1:T(8,128)S(1)} %get-tuple-element.23, pred[512,2048]{1,0:T(8,128)(4,1)S(1)} %bitcast.94), kind=kOutput, calls=%fused_computation.15 | convolution fusion | flops 1368391680 | bytes 25962496 | tf_op jit(solution)/shard_map/qhk,khd->qhd/dot_general | solution.py:73
  181.0 5.2 %convolution_convert_fusion.1 = bf16[256,640]{1,0:T(8,128)(2,1)S(1)} fusion(bf16[256,5120]{0,1:T(8,128)(2,1)S(1)} %bitcast.107, bf16[640,5120]{1,0:T(8,128)(2,1)} %param.10), kind=kOutput, calls=%fused_computation.26 | convolution fusion | flops 1677885440 | bytes 9502720 | tf_op jit(solution)/shard_map/dot_general | solution.py:48
  191.7 15.5 %fusion.1 = bf16[512,5,2048]{2,0,1:T(8,128)(2,1)} fusion(f32[5,512,2048]{2,1,0:T(8,128)} %copy-done, f32[512,5]{0,1:T(8,128)S(1)} %get-tuple-element.20, f32[512,5]{0,1:T(8,128)S(1)} %get-tuple-element.19, pred[512,2048]{1,0:T(8,128)(4,1)S(1)} %bitcast.95, bf16[512,5,128]{0,2,1:T(8,128)(2,1)S(1)} %bitcast.115, bf16[2048,5,128]{0,2,1:T(8,128)(2,1)} %bitcast.106), kind=kOutput, calls=%fused_computation.4 | convolution fusion | flops 1373634560 | bytes 35803136 | tf_op jit(solution)/shard_map/qhd,khd->qhk/dot_general | solution.py:105
  207.2 7.1 %multiply_convert_fusion = bf16[5,128,2048]{2,1,0:T(8,128)(2,1)} fusion(bf16[512,5,128]{0,2,1:T(8,128)(2,1)S(1)} %bitcast.101, bf16[512,5,2048]{2,0,1:T(8,128)(2,1)} %fusion.1), kind=kOutput, calls=%fused_computation.19 | convolution fusion | flops 1344798720 | bytes 13762560 | tf_op jit(solution)/shard_map/qhk,qhd->khd/dot_general | solution.py:113
  214.3 4.4 %copy.77 = bf16[2048,640]{1,0:T(8,128)(2,1)} copy(bf16[2048,640]{0,1:T(8,128)(2,1)} %bitcast.97) | data formatting | bytes 5242880 | tf_op jit(solution)/shard_map/reshape | solution.py:118
  219.0 11.4 %fusion.14 = bf16[5,128,2048]{2,1,0:T(8,128)(2,1)} fusion(bf16[512,5,128]{0,2,1:T(8,128)(2,1)S(1)} %bitcast.116, f32[5,512,2048]{2,1,0:T(8,128)} %copy-done, f32[512,5]{0,1:T(8,128)S(1)} %get-tuple-element.19, pred[512,2048]{1,0:T(8,128)(4,1)S(1)} %bitcast.96), kind=kOutput, calls=%fused_computation.21 | convolution fusion | flops 1364459520 | bytes 25307136 | tf_op jit(solution)/shard_map/qhk,qhd->khd/dot_general | solution.py:115
  230.4 4.4 %copy.78 = bf16[2048,640]{1,0:T(8,128)(2,1)} copy(bf16[2048,640]{0,1:T(8,128)(2,1)} %bitcast.108) | data formatting | bytes 5242880 | tf_op jit(solution)/shard_map/reshape | solution.py:119
  234.9 5.1 %convolution_convert_fusion = bf16[256,5120]{1,0:T(8,128)(2,1)S(1)} fusion(bf16[256,640]{0,1:T(8,128)(2,1)S(1)} %get-tuple-element.13, bf16[640,5120]{1,0:T(8,128)(2,1)} %param.10), kind=kOutput, calls=%fused_computation.18 | convolution fusion | flops 1679032320 | bytes 9502720 | tf_op jit(solution)/shard_map/dot_general | solution.py:90
  241.8 6.5 %all-to-all-start = ((bf16[256,8,640]{2,0,1:T(8,128)(2,1)}), bf16[256,8,640]{2,0,1:T(8,128)(2,1)S(1)}, u32[]{:S(2)}, u32[]{:S(2)}) async-start(bf16[256,8,640]{2,0,1:T(8,128)(2,1)} %bitcast.98), calls=%async_computation | async-start | bytes 5242880 | tf_op jit(solution)/shard_map/all_to_all | solution.py:91
  248.3 8.4 %fusion.17 = f32[512,5,128]{0,2,1:T(8,128)S(1)} fusion(bf16[512,5,2048]{2,0,1:T(8,128)(2,1)} %fusion.1, bf16[2048,5,128]{0,2,1:T(8,128)(2,1)} %bitcast.103), kind=kOutput, calls=%fused_computation.24 | convolution fusion | flops 1342504960 | bytes 14417920 | tf_op jit(solution)/shard_map/qhk,khd->qhd/dot_general | solution.py:108
  263.1 44.3 %all-to-all-done = bf16[256,8,640]{2,0,1:T(8,128)(2,1)S(1)} async-done(((bf16[256,8,640]{2,0,1:T(8,128)(2,1)}), bf16[256,8,640]{2,0,1:T(8,128)(2,1)S(1)}, u32[]{:S(2)}, u32[]{:S(2)}) %all-to-all-start) | async-done | bytes 2621472 | tf_op jit(solution)/shard_map/all_to_all | solution.py:91
  308.6 64.5 %reduce-scatter.5.cloned.1.call-done = bf16[256,640]{1,0:T(8,128)(2,1)} async-done(((bf16[2048,640]{1,0:T(8,128)(2,1)}), bf16[256,640]{1,0:T(8,128)(2,1)}) %reduce-scatter.5.cloned.1.call-update) | async-done | bytes 327696 | tf_op jit(solution)/shard_map/reduce_scatter | solution.py:119
  (65 shorter events, 20.7 us)
Async XLA Ops:
  7.2 13.4 %copy-start.3 = (bf16[256,640]{1,0:T(8,128)(2,1)S(1)}, bf16[256,640]{1,0:T(8,128)(2,1)}, u32[]{:S(2)}) copy-start(bf16[256,640]{1,0:T(8,128)(2,1)} %param.7) | copy-start | bytes 983044
  7.2 13.6 %copy-start.4 = (s32[32,32]{1,0:T(8,128)S(1)}, s32[32,32]{1,0:T(8,128)}, u32[]{:S(2)}) copy-start(s32[32,32]{1,0:T(8,128)} %param.12) | copy-start | bytes 12292
  7.2 13.6 %copy-start.5 = (s32[32]{0:T(128)S(1)}, s32[32]{0:T(128)}, u32[]{:S(2)}) copy-start(s32[32]{0:T(128)} %param.13) | copy-start | bytes 388
  7.2 91.5 %all-gather.3.cloned.1.call-start = ((), (), s32[]{:S(2)}) async-start(), calls=%async_computation.4 | async-start | bytes 2949120 | tf_op jit(solution)/shard_map/all_gather | solution.py:52
  11.9 68.1 %all-to-all-start.1 = ((bf16[256,8,640]{2,0,1:T(8,128)(2,1)}), bf16[256,8,640]{2,0,1:T(8,128)(2,1)}, u32[]{:S(2)}, u32[]{:S(2)}) async-start(bf16[256,8,640]{2,0,1:T(8,128)(2,1)} %broadcast_in_dim.54), calls=%async_computation.1 | async-start | bytes 5242880 | tf_op jit(solution)/shard_map/all_to_all | solution.py:47
  19.8 144.5 %all-gather.5.cloned.1.call-start = ((), (), s32[]{:S(2)}) async-start(), calls=%async_computation.5 | async-start | bytes 2949120 | tf_op jit(solution)/shard_map/all_gather | solution.py:53
  20.5 288.1 %reduce-scatter.3.cloned.1.call-start = ((), (), s32[]{:S(2)}) async-start(), calls=%async_computation.6 | async-start | bytes 2949120 | tf_op jit(solution)/shard_map/reduce_scatter | solution.py:118
  20.6 5.9 %collective-permute-start = (bf16[256,640]{1,0:T(8,128)(2,1)S(1)}, bf16[256,640]{1,0:T(8,128)(2,1)S(1)}, u32[]{:S(2)}, u32[]{:S(2)}) collective-permute-start(bf16[256,640]{1,0:T(8,128)(2,1)S(1)} %copy-done.3), channel_id=1, source_target_pairs={{0,8},{8,0},{1,9},{9,1},{2,10},{10,2},{3,11},{11,3},{4,12},{12,4},... | collective-permute-start | bytes 983048 | tf_op jit(solution)/shard_map/ppermute | solution.py:16
  104.8 7.0 %copy-start = (f32[5,512,2048]{2,1,0:T(8,128)}, f32[5,512,2048]{2,1,0:T(8,128)S(1)}, u32[]{:S(2)}) copy-start(f32[5,512,2048]{2,1,0:T(8,128)S(1)} %get-tuple-element.24) | copy-start | bytes 62914564
  168.8 12.2 %copy-start.2 = (bf16[256,8,640]{0,2,1:T(8,128)(2,1)S(1)}, bf16[256,8,640]{0,2,1:T(8,128)(2,1)}, u32[]{:S(2)}) copy-start(bf16[256,8,640]{0,2,1:T(8,128)(2,1)} %copy.70) | copy-start | bytes 7864324
  180.9 7.1 %collective-permute-start.1 = (f32[256,650]{0,1:T(8,128)}, f32[256,650]{0,1:T(8,128)}, u32[]{:S(2)}, u32[]{:S(2)}) collective-permute-start(f32[256,650]{0,1:T(8,128)} %get-tuple-element.9), channel_id=1, source_target_pairs={{0,8},{8,0},{1,9},{9,1},{2,10},{10,2},{3,11},{11,3},{4,12},{12,4},... | collective-permute-start | bytes 1996808 | tf_op jit(solution)/shard_map/ppermute | solution.py:16
  186.1 1.8 collective-permute-start.3
  190.4 1.3 collective-permute-start.2
  191.7 15.5 %copy-start.1 = (bf16[512,640]{0,1:T(8,128)(2,1)S(1)}, bf16[512,640]{0,1:T(8,128)(2,1)}, u32[]{:S(2)}) copy-start(bf16[512,640]{0,1:T(8,128)(2,1)} %copy.64) | copy-start | bytes 1966084
  218.8 154.3 %reduce-scatter.5.cloned.1.call-start = ((), (), s32[]{:S(2)}) async-start(), calls=%async_computation.7 | async-start | bytes 2949120 | tf_op jit(solution)/shard_map/reduce_scatter | solution.py:119
  241.8 65.7 %all-to-all-start = ((bf16[256,8,640]{2,0,1:T(8,128)(2,1)}), bf16[256,8,640]{2,0,1:T(8,128)(2,1)S(1)}, u32[]{:S(2)}, u32[]{:S(2)}) async-start(bf16[256,8,640]{2,0,1:T(8,128)(2,1)} %bitcast.98), calls=%async_computation | async-start | bytes 5242880 | tf_op jit(solution)/shard_map/all_to_all | solution.py:91
  258.8 2.4 collective-permute-start.4
Sparse Core Ops, SparseCore 0:
  10.1 88.4 all-gather.2
  100.3 63.9 all-gather.4
  218.9 89.6 reduce-scatter.2
  311.4 61.6 reduce-scatter.4

commit v2 on v1

--- a/solution.py
+++ b/solution.py
@@ -43,14 +43,16 @@
     allowed = jnp.logical_or(chains[:, None] == chains[None, :], contacts > 0)
     q_blocks = rows // BLOCK
 
-    spread = jnp.broadcast_to(cotangent[:, None, :], (rows, n_head, width))
-    full_cotangent = lax.all_to_all(spread, "head", 1, 1, tiled=True).reshape(rows, n_head * width)
+    full_cotangent = lax.all_gather(cotangent, "head", axis=1, tiled=True)
     grads = lax.dot_general(
         full_cotangent, out_weight, (((1,), (1,)), ((), ())), preferred_element_type=jnp.float32
     ).astype(jnp.bfloat16)
 
-    key_half = lax.all_gather(keys, "ctxo", axis=0, tiled=True)
-    value_half = lax.all_gather(values, "ctxo", axis=0, tiled=True)
+    pair = jnp.concatenate([keys, values], axis=1)
+    spread = jnp.broadcast_to(pair[None], (n_out,) + pair.shape)
+    gathered = lax.all_to_all(spread, "ctxo", 0, 0, tiled=True)
+    key_half = gathered[:, :, :width].reshape(n_out * rows, width)
+    value_half = gathered[:, :, width:].reshape(n_out * rows, width)
     count = key_half.shape[0]
 
     q_chip = pair_rows(queries, swap(queries), core)
@@ -115,8 +117,12 @@
     value_part = jnp.einsum(
         "qhk,qhd->khd", probs.astype(jnp.bfloat16), g_chip, preferred_element_type=jnp.float32
     ).astype(jnp.bfloat16)
-    key_grad = lax.psum_scatter(key_part.reshape(count, width), "ctxo", scatter_dimension=0, tiled=True)
-    value_grad = lax.psum_scatter(value_part.reshape(count, width), "ctxo", scatter_dimension=0, tiled=True)
+    grad_parts = jnp.concatenate(
+        [key_part.reshape(count, width), value_part.reshape(count, width)], axis=1
+    ).reshape(n_out, rows, 2 * width)
+    summed = jnp.sum(lax.all_to_all(grad_parts, "ctxo", 0, 0, tiled=True).astype(jnp.float32), axis=0)
+    key_grad = summed[:, :width].astype(jnp.bfloat16)
+    value_grad = summed[:, width:].astype(jnp.bfloat16)
     return (mixed, query_grad, key_grad, value_grad)
 
 

time: 381 us -> 296 us (0.78)
  waiting for transfers between devices: 224 us -> 127 us
  other arithmetic: 14.6 us -> 28.5 us
  local copies, waits for them, and re-layouts: 40.7 us -> 35.8 us
    all_to_all x1 -> x2, waiting for transfers between devices: 52.2 us -> 125 us  [the longest x1 75.5 us: per_device(): gathered = lax.all_to_all(spread, 'ctxo', 0, 0, tiled=True)]
    reduce_scatter x2 -> x0, waiting for transfers between devices: 64.5 us -> none  [the longest x1 64.5 us: per_device(): lax.psum_scatter(value_part.reshape(count, width), 'ctxo', scatter_dimens...]
    all_gather x2 -> x1, waiting for transfers between devices: 59.9 us -> 0.01 us  [per_device(): full_cotangent = lax.all_gather(cotangent, 'head', axis=1, tiled=True)]
    all_to_all x1, waiting for transfers between devices: 44.3 us -> 0.01 us  [per_device(): lax.all_to_all(projected.astype(jnp.bfloat16).reshape(rows, n_head, width...]
    another operation x0 -> x2, local copies, waits for them, and re-layouts: none -> 9.12 us  [the longest x1 5.24 us: per_device(): v_three = value_half.reshape(count, heads, size)]
    slice x0 -> x4, local copies, waits for them, and re-layouts: none -> 9.03 us  [the longest x2 5.94 us: per_device(): key_half = gathered[:, :, :width].reshape(n_out * rows, width)]
    reshape x2 -> x0, local copies, waits for them, and re-layouts: 8.81 us -> none  [the longest x1 4.41 us: per_device(): key_part.reshape(count, width)]
    unnamed x14 -> x21, local copies, waits for them, and re-layouts: 9.6 us -> 3.88 us
  transfers between devices with their start and end apart: 11 -> 9, of which waited for: 8 -> 3; matrix products, arithmetic and copies ran while one was open for 18% -> 39% of each run, Pallas kernels for 0% -> 0%
where the time goes in v2:
time: 296 us; the launch traced here: 294 us
  waiting for transfers between devices  127 us (43%)
  matrix products  69.5 us (23%)
  local copies, waits for them, and re-layouts  35.8 us (12%)
  other arithmetic  28.5 us (10%)
  starting transfers between devices  19.1 us (6%)
  between operations  14.4 us (5%)
    all_to_all x1, waiting for transfers between devices, per_device(): gathered = lax.all_to_all(spread, 'ctxo', 0, 0, tiled=True)  75.5 us
    all_to_all x1, waiting for transfers between devices, per_device(): lax.all_to_all(grad_parts, 'ctxo', 0, 0, tiled=True).astype(jnp.float32)  49.3 us
    dot_general x1, matrix products, per_device(): jnp.einsum('qhd,khd->qhk', g_chip, v_three, preferred_element_type=jnp.fl...  14.4 us
    dot_general x1, matrix products, per_device(): jnp.einsum('qhk,khd->qhd', weights.astype(jnp.bfloat16), v_three, preferr...  11.3 us
    reduce_sum x1, other arithmetic, per_device(): total = jnp.sum(weights, axis=2)  10 us
    dot_general x1, matrix products, per_device(): jnp.einsum('qhk,qhd->khd', probs.astype(jnp.bfloat16), g_chip, preferred_...  9.89 us
    dot_general x1, matrix products, per_device(): jnp.einsum('qhd,khd->qhk', q_three, k_three, preferred_element_type=jnp.f...  9.12 us
    all_to_all x1, starting transfers between devices, per_device(): lax.all_to_all(projected.astype(jnp.bfloat16).reshape(rows, n_head, width...  7.48 us
  transfers between devices with their start and end apart: 9, of which 3 were waited for; matrix products, arithmetic and copies ran while one was open for 39% of the time, Pallas kernels for 0%

profile of v2, /device:TPU:0, one launch (start us, length us, event | category | flops | bytes accessed | tf_op | source)
XLA Modules:
  0.0 294.3 jit_solution(5845266818587381798)
XLA Ops:
  8.5 2.7 broadcast_in_dim.52
  11.2 5.6 %all-to-all-start = ((bf16[8,256,1280]{1,2,0:T(8,128)(2,1)}), bf16[8,256,1280]{1,2,0:T(8,128)(2,1)}, u32[]{:S(2)}, u32[]{:S(2)}) async-start(bf16[8,256,1280]{1,2,0:T(8,128)(2,1)} %broadcast_in_dim.52), calls=%async_computation | async-start | bytes 10485760 | tf_op jit(solution)/shard_map/all_to_all | solution.py:53
  19.7 75.5 %all-to-all-done = bf16[8,256,1280]{1,2,0:T(8,128)(2,1)} async-done(((bf16[8,256,1280]{1,2,0:T(8,128)(2,1)}), bf16[8,256,1280]{1,2,0:T(8,128)(2,1)}, u32[]{:S(2)}, u32[]{:S(2)}) %all-to-all-start) | async-done | bytes 5242912 | tf_op jit(solution)/shard_map/all_to_all | solution.py:53
  95.2 2.9 fusion.30
  98.1 3.0 %copy.53 = bf16[8,256,640]{1,0,2:T(8,128)(2,1)} copy(bf16[8,256,640]{1,2,0:T(8,128)(2,1)S(1)} %get-tuple-element.13) | data formatting | bytes 5242880 | tf_op jit(solution)/shard_map/slice | solution.py:55
  101.2 5.2 %reshape_reshape.7 = bf16[2048,5,128]{0,2,1:T(8,128)(2,1)} reshape(bf16[8,256,640]{1,0,2:T(8,128)(2,1)} %copy.53) | data formatting | bytes 5242880 | tf_op jit(solution)/shard_map/reshape;reshape | solution.py:62
  106.4 3.0 %copy.49 = bf16[8,256,640]{1,0,2:T(8,128)(2,1)} copy(bf16[8,256,640]{1,2,0:T(8,128)(2,1)S(1)} %get-tuple-element.12) | data formatting | bytes 5242880 | tf_op jit(solution)/shard_map/slice | solution.py:54
  109.4 3.9 %reshape_reshape.6 = bf16[2048,5,128]{0,2,1:T(8,128)(2,1)S(1)} reshape(bf16[8,256,640]{1,0,2:T(8,128)(2,1)} %copy.49) | data formatting | bytes 5242880 | tf_op jit(solution)/shard_map/reshape;reshape | solution.py:61
  113.6 9.1 %fusion.4 = (f32[512,5]{0,1:T(8,128)S(1)}, f32[5,2048,512]{2,1,0:T(8,128)}) fusion(pred[512,2048]{0,1:T(8,128)(4,1)S(1)} %bitcast.101, bf16[2048,5,128]{0,2,1:T(8,128)(2,1)S(1)} %reshape_reshape.6, bf16[512,5,128]{0,2,1:T(8,128)(2,1)S(1)} %bitcast.111), kind=kOutput, calls=%fused_computation.10 | convolution fusion | flops 1357903360 | bytes 25307136 | tf_op jit(solution)/shard_map/qhd,khd->qhk/dot_general | solution.py:70
  122.7 10.0 %fusion.7 = f32[512,5]{0,1:T(8,128)S(1)} fusion(f32[5,2048,512]{2,1,0:T(8,128)} %get-tuple-element.32, f32[512,5]{0,1:T(8,128)S(1)} %get-tuple-element.31, pred[512,2048]{0,1:T(8,128)(4,1)S(1)} %bitcast.102), kind=kLoop, calls=%fused_computation.13 | loop fusion | flops 26211840 | bytes 22040576 | tf_op jit(solution)/shard_map/reduce_sum | solution.py:74
  132.8 11.3 %fusion.10 = f32[5,128,512]{2,1,0:T(8,128)} fusion(bf16[2048,5,128]{0,2,1:T(8,128)(2,1)S(1)} %copy-done.3, f32[5,2048,512]{2,1,0:T(8,128)} %get-tuple-element.32, f32[512,5]{0,1:T(8,128)S(1)} %get-tuple-element.31, pred[512,2048]{0,1:T(8,128)(4,1)S(1)} %bitcast.103), kind=kOutput, calls=%fused_computation.15 | convolution fusion | flops 1368391680 | bytes 25962496 | tf_op jit(solution)/shard_map/qhk,khd->qhd/dot_general | solution.py:75
  144.0 6.7 %convolution_convert_fusion.1 = bf16[256,640]{1,0:T(8,128)(2,1)} fusion(bf16[256,5120]{1,0:T(8,128)(2,1)} %all-gather.2.cloned.1.call-done, bf16[640,5120]{1,0:T(8,128)(2,1)} %param.10), kind=kOutput, calls=%fused_computation.26 | convolution fusion | flops 1677885440 | bytes 9502720 | tf_op jit(solution)/shard_map/dot_general | solution.py:47
  156.7 2.2 copy.57
  162.5 5.1 %convolution_convert_fusion = bf16[256,5120]{1,0:T(8,128)(2,1)S(1)} fusion(bf16[256,640]{0,1:T(8,128)(2,1)S(1)} %get-tuple-element.19, bf16[640,5120]{1,0:T(8,128)(2,1)} %param.10), kind=kOutput, calls=%fused_computation.18 | convolution fusion | flops 1679032320 | bytes 9502720 | tf_op jit(solution)/shard_map/dot_general | solution.py:92
  169.3 7.5 %all-to-all-start.1 = ((bf16[256,8,640]{2,0,1:T(8,128)(2,1)}), bf16[256,8,640]{2,0,1:T(8,128)(2,1)}, u32[]{:S(2)}, u32[]{:S(2)}) async-start(bf16[256,8,640]{2,0,1:T(8,128)(2,1)} %bitcast.106), calls=%async_computation.1 | async-start | bytes 5242880 | tf_op jit(solution)/shard_map/all_to_all | solution.py:93
  176.8 9.9 %fusion.14 = bf16[5,128,2048]{2,1,0:T(8,128)(2,1)S(1)} fusion(bf16[512,5,128]{0,2,1:T(8,128)(2,1)} %bitcast.120, f32[5,2048,512]{2,1,0:T(8,128)} %get-tuple-element.32, f32[512,5]{0,1:T(8,128)S(1)} %get-tuple-element.27, pred[512,2048]{0,1:T(8,128)(4,1)} %bitcast.104), kind=kOutput, calls=%fused_computation.21 | convolution fusion | flops 1364459520 | bytes 25307136 | tf_op jit(solution)/shard_map/qhk,qhd->khd/dot_general | solution.py:117
  189.6 14.4 %fusion.1 = bf16[512,5,2048]{0,2,1:T(8,128)(2,1)} fusion(f32[5,2048,512]{2,1,0:T(8,128)} %get-tuple-element.32, f32[512,5]{0,1:T(8,128)S(1)} %get-tuple-element.28, f32[512,5]{0,1:T(8,128)S(1)} %get-tuple-element.27, pred[512,2048]{0,1:T(8,128)(4,1)S(1)} %bitcast.105, bf16[2048,5,128]{0,2,1:T(8,128)(2,1)} %reshape_reshape.7, bf16[512,5,128]{0,2,1:T(8,128)(2,1)} %bitcast.121), kind=kOutput, calls=%fused_computation.4 | convolution fusion | flops 1373634560 | bytes 35803136 | tf_op jit(solution)/shard_map/qhd,khd->qhk/dot_general | solution.py:107
  204.1 7.5 %multiply_convert_fusion = bf16[5,128,2048]{2,1,0:T(8,128)(2,1)S(1)} fusion(bf16[512,5,128]{0,2,1:T(8,128)(2,1)S(1)} %bitcast.112, bf16[512,5,2048]{0,2,1:T(8,128)(2,1)} %fusion.1), kind=kOutput, calls=%fused_computation.20 | convolution fusion | flops 1344798720 | bytes 13762560 | tf_op jit(solution)/shard_map/qhk,qhd->khd/dot_general | solution.py:115
  213.3 2.6 pad_maximum_fusion
  215.9 4.9 %all-to-all-start.2 = ((bf16[8,256,1280]{1,2,0:T(8,128)(2,1)}), bf16[8,256,1280]{1,2,0:T(8,128)(2,1)}, u32[]{:S(2)}, u32[]{:S(2)}) async-start(bf16[8,256,1280]{1,2,0:T(8,128)(2,1)} %pad_maximum_fusion), calls=%async_computation.2 | async-start | bytes 10485760 | tf_op jit(solution)/shard_map/all_to_all | solution.py:123
  220.9 5.5 %fusion.17 = f32[512,5,128]{0,2,1:T(8,128)S(1)} fusion(bf16[2048,5,128]{0,2,1:T(8,128)(2,1)S(1)} %reshape_reshape.6, bf16[512,5,2048]{0,2,1:T(8,128)(2,1)} %fusion.1), kind=kOutput, calls=%fused_computation.24 | convolution fusion | flops 1342504960 | bytes 14417920 | tf_op jit(solution)/shard_map/qhk,khd->qhd/dot_general | solution.py:110
  229.7 2.9 reduce_sum.40
  232.6 49.3 %all-to-all-done.2 = bf16[8,256,1280]{1,2,0:T(8,128)(2,1)} async-done(((bf16[8,256,1280]{1,2,0:T(8,128)(2,1)}), bf16[8,256,1280]{1,2,0:T(8,128)(2,1)}, u32[]{:S(2)}, u32[]{:S(2)}) %all-to-all-start.2) | async-done | bytes 5242912 | tf_op jit(solution)/shard_map/all_to_all | solution.py:123
  282.0 3.6 %reduce.1 = bf16[256,1280]{0,1:T(8,128)(2,1)S(1)} reduce(bf16[8,256,1280]{1,2,0:T(8,128)(2,1)} %all-to-all-done.2, bf16[]{:T(256)} %constant.12.clone.1), dimensions={0}, to_apply=%region_4.5.clone | reduce | flops 2293760 | bytes 5898242 | tf_op jit(solution)/shard_map/reduce_sum | solution.py:123
  (72 shorter events, 25.4 us)
Async XLA Ops:
  11.2 5.7 %copy-start.5 = (bf16[256,640]{1,0:T(8,128)(2,1)S(1)}, bf16[256,640]{1,0:T(8,128)(2,1)}, u32[]{:S(2)}) copy-start(bf16[256,640]{1,0:T(8,128)(2,1)} %param.7) | copy-start | bytes 983044
  11.2 6.4 %copy-start.6 = (s32[32,32]{1,0:T(8,128)S(1)}, s32[32,32]{1,0:T(8,128)}, u32[]{:S(2)}) copy-start(s32[32,32]{1,0:T(8,128)} %param.12) | copy-start | bytes 12292
  11.2 6.4 %copy-start.7 = (s32[32]{0:T(128)S(1)}, s32[32]{0:T(128)}, u32[]{:S(2)}) copy-start(s32[32]{0:T(128)} %param.13) | copy-start | bytes 388
  11.2 83.9 %all-to-all-start = ((bf16[8,256,1280]{1,2,0:T(8,128)(2,1)}), bf16[8,256,1280]{1,2,0:T(8,128)(2,1)}, u32[]{:S(2)}, u32[]{:S(2)}) async-start(bf16[8,256,1280]{1,2,0:T(8,128)(2,1)} %broadcast_in_dim.52), calls=%async_computation | async-start | bytes 10485760 | tf_op jit(solution)/shard_map/all_to_all | solution.py:53
  16.9 127.2 %all-gather.2.cloned.1.call-start = ((), (), s32[]{:S(2)}) async-start(), calls=%async_computation.3 | async-start | bytes 2949120 | tf_op jit(solution)/shard_map/all_gather | solution.py:46
  16.9 2.3 collective-permute-start
  113.6 19.2 %copy-start = (pred[512,16,128]{0,2,1:T(8,128)(4,1)}, pred[512,16,128]{0,2,1:T(8,128)(4,1)S(1)}, u32[]{:S(2)}) copy-start(pred[512,16,128]{0,2,1:T(8,128)(4,1)S(1)} %broadcast_in_dim.49) | copy-start | bytes 3145732
  122.7 10.1 %copy-start.3 = (bf16[2048,5,128]{0,2,1:T(8,128)(2,1)S(1)}, bf16[2048,5,128]{0,2,1:T(8,128)(2,1)}, u32[]{:S(2)}) copy-start(bf16[2048,5,128]{0,2,1:T(8,128)(2,1)} %reshape_reshape.7) | copy-start | bytes 7864324
  144.0 6.7 %copy-start.4 = (f32[5,128,512]{2,1,0:T(8,128)S(1)}, f32[5,128,512]{2,1,0:T(8,128)}, u32[]{:S(2)}) copy-start(f32[5,128,512]{2,1,0:T(8,128)} %fusion.10) | copy-start | bytes 3932164
  150.8 3.9 %collective-permute-start.3 = (bf16[256,640]{1,0:T(8,128)(2,1)}, bf16[256,640]{1,0:T(8,128)(2,1)}, u32[]{:S(2)}, u32[]{:S(2)}) collective-permute-start(bf16[256,640]{1,0:T(8,128)(2,1)} %convolution_convert_fusion.1), channel_id=1, source_target_pairs={{0,8},{8,0},{1,9},{9,1},{2,10},{10,2},{3,11},{11,3},{4,12},{12,4},... | collective-permute-start | bytes 983048 | tf_op jit(solution)/shard_map/ppermute | solution.py:16
  152.1 6.7 %collective-permute-start.1 = (f32[256,650]{0,1:T(8,128)}, f32[256,650]{0,1:T(8,128)}, u32[]{:S(2)}, u32[]{:S(2)}) collective-permute-start(f32[256,650]{0,1:T(8,128)} %get-tuple-element.15), channel_id=1, source_target_pairs={{0,8},{8,0},{1,9},{9,1},{2,10},{10,2},{3,11},{11,3},{4,12},{12,4},... | collective-permute-start | bytes 1996808 | tf_op jit(solution)/shard_map/ppermute | solution.py:16
  162.4 14.4 %collective-permute-start.2 = (f32[256,10]{0,1:T(8,128)S(1)}, f32[256,10]{0,1:T(8,128)S(1)}, u32[]{:S(2)}, u32[]{:S(2)}) collective-permute-start(f32[256,10]{0,1:T(8,128)S(1)} %pad_maximum_fusion.6), channel_id=1, source_target_pairs={{0,8},{8,0},{1,9},{9,1},{2,10},{10,2},{3,11},{11,3},{4,12},{12,4},... | collective-permute-start | bytes 30728 | tf_op jit(solution)/shard_map/ppermute | solution.py:16
  169.3 46.6 %all-to-all-start.1 = ((bf16[256,8,640]{2,0,1:T(8,128)(2,1)}), bf16[256,8,640]{2,0,1:T(8,128)(2,1)}, u32[]{:S(2)}, u32[]{:S(2)}) async-start(bf16[256,8,640]{2,0,1:T(8,128)(2,1)} %bitcast.106), calls=%async_computation.1 | async-start | bytes 5242880 | tf_op jit(solution)/shard_map/all_to_all | solution.py:93
  186.7 2.9 copy-start.1
  211.5 1.7 copy-start.2
  215.9 66.0 %all-to-all-start.2 = ((bf16[8,256,1280]{1,2,0:T(8,128)(2,1)}), bf16[8,256,1280]{1,2,0:T(8,128)(2,1)}, u32[]{:S(2)}, u32[]{:S(2)}) async-start(bf16[8,256,1280]{1,2,0:T(8,128)(2,1)} %pad_maximum_fusion), calls=%async_computation.2 | async-start | bytes 10485760 | tf_op jit(solution)/shard_map/all_to_all | solution.py:123
  226.8 2.2 collective-permute-start.4
Sparse Core Ops, SparseCore 0:
  20.1 78.3 all-gather.1

commit v3 on v1

v3 whole, which is shorter than its diff:
```python
import jax
import jax.numpy as jnp
from jax import lax
from jax.sharding import Mesh
from jax.sharding import PartitionSpec as P

HEAD_SIZE = 128
BLOCK = 128

NEG = -1e30
CTX = ("ctxo", "core")
SWAP = [(0, 1), (1, 0)]


def swap(value):
    return lax.ppermute(value, "core", SWAP)


def shift(value, step, count):
    return lax.ppermute(value, "ctxo", [(i, (i + step) % count) for i in range(count)])


def pair_rows(own, other, core):
    first = jnp.where(core == 0, own, other)
    second = jnp.where(core == 0, other, own)
    return jnp.concatenate([first, second], axis=0)


def halves(value, core):
    rows = value.shape[0] // 2
    top, bottom = value[:rows], value[rows:]
    own = jnp.where(core == 0, top, bottom)
    other = jnp.where(core == 0, bottom, top)
    return own, other


def per_device(queries, keys, values, out_weight, cotangent, contacts, chains):
    scale = HEAD_SIZE ** (-0.5)
    rows = queries.shape[0]
    size = HEAD_SIZE
    heads = queries.shape[1] // size
    width = heads * size
    n_out = lax.axis_size("ctxo")
    n_head = lax.axis_size("head")
    core = lax.axis_index("core")
    outer = lax.axis_index("ctxo")
    allowed = jnp.logical_or(chains[:, None] == chains[None, :], contacts > 0)
    q_blocks = rows // BLOCK
    chip_rows = 2 * rows

    pair = jnp.stack([keys, values])
    shards = [pair] + [shift(pair, s, n_out) for s in range(1, n_out)]

    full_cotangent = lax.all_gather(cotangent, "head", axis=1, tiled=True)
    grads = lax.dot_general(
        full_cotangent, out_weight, (((1,), (1,)), ((), ())), preferred_element_type=jnp.float32
    ).astype(jnp.bfloat16)

    q_three = pair_rows(queries, swap(queries), core).reshape(chip_rows, heads, size)

    row_blocks = outer * (2 * q_blocks) + jnp.arange(2 * q_blocks)
    row_mask = allowed[row_blocks]

    def keep_of(s):
        source = (outer - s) % n_out
        cols = (2 * source + core) * q_blocks + jnp.arange(q_blocks)
        part = row_mask[:, cols]
        return jnp.repeat(jnp.repeat(part, BLOCK, axis=0), BLOCK, axis=1)[:, None, :]

    keeps = [keep_of(s) for s in range(n_out)]

    best = jnp.full((chip_rows, heads), NEG, jnp.float32)
    total = jnp.zeros((chip_rows, heads), jnp.float32)
    accum = jnp.zeros((chip_rows, heads, size), jnp.float32)
    for s in range(n_out):
        k_three = shards[s][0].reshape(rows, heads, size)
        v_three = shards[s][1].reshape(rows, heads, size)
        keep = keeps[s]
        scores = jnp.einsum("qhd,khd->qhk", q_three, k_three, preferred_element_type=jnp.float32) * scale
        scores = jnp.where(keep, scores, NEG)
        best_new = jnp.maximum(best, jnp.max(scores, axis=2))
        weights = jnp.where(keep, jnp.exp(scores - best_new[:, :, None]), 0.0)
        fix = jnp.exp(best - best_new)
        total = total * fix + jnp.sum(weights, axis=2)
        accum = accum * fix[:, :, None] + jnp.einsum(
            "qhk,khd->qhd", weights.astype(jnp.bfloat16), v_three, preferred_element_type=jnp.float32
        )
        best = best_new

    state = jnp.concatenate([best, total, accum.reshape(chip_rows, width)], axis=1)
    own_state, other_state = halves(state, core)
    got_state = swap(other_state)
    best_a, total_a, acc_a = own_state[:, :heads], own_state[:, heads:2 * heads], own_state[:, 2 * heads:]
    best_b, total_b, acc_b = got_state[:, :heads], got_state[:, heads:2 * heads], got_state[:, 2 * heads:]
    best_m = jnp.maximum(best_a, best_b)
    fa = jnp.exp(best_a - best_m)
    fb = jnp.exp(best_b - best_m)
    total_m = total_a * fa + total_b * fb
    acc_m = acc_a.reshape(rows, heads, size) * fa[:, :, None] + acc_b.reshape(rows, heads, size) * fb[:, :, None]
    attended = (acc_m / total_m[:, :, None]).astype(jnp.bfloat16)
    lse = best_m + jnp.log(total_m)

    projected = jnp.dot(attended.reshape(rows, width), out_weight, preferred_element_type=jnp.float32)
    parts = lax.all_to_all(
        projected.astype(jnp.bfloat16).reshape(rows, n_head, width), "head", 1, 1, tiled=True
    )
    mixed = jnp.sum(parts.astype(jnp.float32), axis=1).astype(jnp.bfloat16)

    g_own = grads.reshape(rows, heads, size)
    delta = jnp.sum(g_own.astype(jnp.float32) * attended.astype(jnp.float32), axis=2)
    side = jnp.concatenate([lse, delta], axis=1)
    side_chip = pair_rows(side, swap(side), core)
    lse_chip, delta_chip = side_chip[:, :heads], side_chip[:, heads:]
    g_three = pair_rows(grads, swap(grads), core).reshape(chip_rows, heads, size)

    q_accum = jnp.zeros((chip_rows, heads, size), jnp.float32)
    kv_sum = None
    for s in range(n_out):
        k_three = shards[s][0].reshape(rows, heads, size)
        v_three = shards[s][1].reshape(rows, heads, size)
        keep = keeps[s]
        scores = jnp.einsum("qhd,khd->qhk", q_three, k_three, preferred_element_type=jnp.float32) * scale
        probs = jnp.where(keep, jnp.exp(scores - lse_chip[:, :, None]), 0.0)
        dprob = jnp.einsum("qhd,khd->qhk", g_three, v_three, preferred_element_type=jnp.float32)
        dscore = (probs * (dprob - delta_chip[:, :, None])).astype(jnp.bfloat16)
        q_term = jnp.einsum("qhk,khd->qhd", dscore, k_three, preferred_element_type=jnp.float32) * scale
        q_accum = q_accum + q_term.astype(jnp.bfloat16).astype(jnp.float32)
        key_part = (
            jnp.einsum("qhk,qhd->khd", dscore, q_three, preferred_element_type=jnp.float32) * scale
        ).astype(jnp.bfloat16)
        value_part = jnp.einsum(
            "qhk,qhd->khd", probs.astype(jnp.bfloat16), g_three, preferred_element_type=jnp.float32
        ).astype(jnp.bfloat16)
        term = jnp.stack([key_part.reshape(rows, width), value_part.reshape(rows, width)])
        if s:
            term = shift(term, n_out - s, n_out)
        term = term.astype(jnp.float32)
        kv_sum = term if kv_sum is None else kv_sum + term

    q_own, q_other = halves(q_accum.reshape(chip_rows, width), core)
    query_grad = (q_own + swap(q_other)).astype(jnp.bfloat16)
    key_grad = kv_sum[0].astype(jnp.bfloat16)
    value_grad = kv_sum[1].astype(jnp.bfloat16)
    return (mixed, query_grad, key_grad, value_grad)


def solution(mesh):
    devices = mesh.devices
    n_ctx, n_head = devices.shape
    split = Mesh(devices.reshape(n_ctx // 2, 2, n_head), ("ctxo", "core", "head"))
    rows_spec = P(CTX, "head")
    in_specs = (rows_spec, rows_spec, rows_spec, P("head", None), rows_spec, P(), P())
    out_specs = (rows_spec, rows_spec, rows_spec, rows_spec)
    return jax.shard_map(
        per_device, mesh=split, in_specs=in_specs, out_specs=out_specs, check_vma=False
    )
```

time: 381 us -> 345 us (0.906); the launches traced: 380 us -> 339 us
  waiting for transfers between devices: 224 us -> 115 us
  starting transfers between devices: 16 us -> 53.7 us
  other arithmetic: 14.6 us -> 33.7 us
  local copies, waits for them, and re-layouts: 40.7 us -> 54.2 us
    ppermute x0 -> x14, waiting for transfers between devices: none -> 91.9 us  [shift(): lax.ppermute(value, 'ctxo', [(i, (i + step) % count) for i in range(count)])]
    reduce_scatter x2 -> x0, waiting for transfers between devices: 64.5 us -> none  [the longest x1 64.5 us: per_device(): lax.psum_scatter(value_part.reshape(count, width), 'ctxo', scatter_dimens...]
    all_gather x2 -> x1, waiting for transfers between devices: 59.9 us -> 0.01 us  [per_device(): full_cotangent = lax.all_gather(cotangent, 'head', axis=1, tiled=True)]
    all_to_all x1 -> x0, waiting for transfers between devices: 52.2 us -> none  [per_device(): lax.all_to_all(spread, 'head', 1, 1, tiled=True)]
    ppermute x0 -> x14, starting transfers between devices: none -> 45 us  [shift(): lax.ppermute(value, 'ctxo', [(i, (i + step) % count) for i in range(count)])]
    another operation x0 -> x16, local copies, waits for them, and re-layouts: none -> 27.7 us  [per_device(): jnp.stack([key_part.reshape(rows, width), value_part.reshape(rows, width)])]
    all_to_all x1, waiting for transfers between devices: 44.3 us -> 20.2 us  [per_device(): lax.all_to_all(projected.astype(jnp.bfloat16).reshape(rows, n_head, width...]
    another operation x0 -> x9, other arithmetic: none -> 14.8 us  [the longest x7 11.8 us: per_device(): jnp.stack([key_part.reshape(rows, width), value_part.reshape(rows, width)])]
  transfers between devices with their start and end apart: 11 -> 21, of which waited for: 8 -> 10; matrix products, arithmetic and copies ran while one was open for 18% -> 23% of each run, Pallas kernels for 0% -> 0%
where the time goes in v3:
time: 345 us; the launch traced here: 339 us
  waiting for transfers between devices  115 us (33%)
  matrix products  66.8 us (19%)
  local copies, waits for them, and re-layouts  54.2 us (16%)
  starting transfers between devices  53.7 us (16%)
  other arithmetic  33.7 us (10%)
  between operations  15.9 us (5%)
    ppermute x14, waiting for transfers between devices, shift(): lax.ppermute(value, 'ctxo', [(i, (i + step) % count) for i in range(count)])  91.9 us
    ppermute x14, starting transfers between devices, shift(): lax.ppermute(value, 'ctxo', [(i, (i + step) % count) for i in range(count)])  45 us
    another operation x16, local copies, waits for them, and re-layouts, per_device(): jnp.stack([key_part.reshape(rows, width), value_part.reshape(rows, width)])  27.7 us
    all_to_all x1, waiting for transfers between devices, per_device(): lax.all_to_all(projected.astype(jnp.bfloat16).reshape(rows, n_head, width...  20.2 us
    dot_general x8, matrix products, per_device(): jnp.einsum('qhk,qhd->khd', probs.astype(jnp.bfloat16), g_three, preferred...  14.8 us
    another operation x7, other arithmetic, per_device(): jnp.stack([key_part.reshape(rows, width), value_part.reshape(rows, width)])  11.8 us
    dot_general x8, matrix products, per_device(): jnp.einsum('qhk,khd->qhd', dscore, k_three, preferred_element_type=jnp.fl...  10.6 us
    dot_general x8, matrix products, per_device(): jnp.einsum('qhd,khd->qhk', g_three, v_three, preferred_element_type=jnp.f...  9.71 us
  transfers between devices with their start and end apart: 21, of which 10 were waited for; matrix products, arithmetic and copies ran while one was open for 23% of the time, Pallas kernels for 0%

profile of v3, /device:TPU:0, one launch (start us, length us, event | category | flops | bytes accessed | tf_op | source)
XLA Modules:
  0.0 339.0 jit_solution(10119645415302839897)
XLA Ops:
  9.8 4.1 %collective-permute-start.7 = (bf16[2,256,640]{1,2,0:T(8,128)(2,1)S(1)}, bf16[2,256,640]{1,2,0:T(8,128)(2,1)S(1)}, u32[]{:S(2)}, u32[]{:S(2)}) collective-permute-start(bf16[2,256,640]{1,2,0:T(8,128)(2,1)S(1)} %pad_maximum_fusion.2), channel_id=1, source_target_pairs={{0,112},{16,0},{32,16},{48,32},{64,48},{80,64},{96,80},{112,96},{1... | collective-permute-start | bytes 1966088 | tf_op jit(solution)/shard_map/ppermute | solution.py:20
  15.1 2.9 collective-permute-start.4
  25.7 19.9 %collective-permute-done.6 = bf16[2,256,640]{1,2,0:T(8,128)(2,1)} collective-permute-done((bf16[2,256,640]{1,2,0:T(8,128)(2,1)S(1)}, bf16[2,256,640]{1,2,0:T(8,128)(2,1)}, u32[]{:S(2)}, u32[]{:S(2)}) %collective-permute-start.6) | collective-permute-done | bytes 655392 | tf_op jit(solution)/shard_map/ppermute | solution.py:20
  45.7 25.2 %collective-permute-start.1 = (bf16[2,256,640]{1,2,0:T(8,128)(2,1)S(1)}, bf16[2,256,640]{1,2,0:T(8,128)(2,1)S(1)}, u32[]{:S(2)}, u32[]{:S(2)}) collective-permute-start(bf16[2,256,640]{1,2,0:T(8,128)(2,1)S(1)} %pad_maximum_fusion.2), channel_id=1, source_target_pairs={{0,16},{16,32},{32,48},{48,64},{64,80},{80,96},{96,112},{112,0},{1... | collective-permute-start | bytes 1966088 | tf_op jit(solution)/shard_map/ppermute | solution.py:20
  75.5 15.2 %collective-permute-done.1 = bf16[2,256,640]{1,2,0:T(8,128)(2,1)S(1)} collective-permute-done((bf16[2,256,640]{1,2,0:T(8,128)(2,1)S(1)}, bf16[2,256,640]{1,2,0:T(8,128)(2,1)S(1)}, u32[]{:S(2)}, u32[]{:S(2)}) %collective-permute-start.1) | collective-permute-done | bytes 655392 | tf_op jit(solution)/shard_map/ppermute | solution.py:20
  92.2 10.2 %collective-permute-done.3 = bf16[2,256,640]{1,2,0:T(8,128)(2,1)S(1)} collective-permute-done((bf16[2,256,640]{1,2,0:T(8,128)(2,1)S(1)}, bf16[2,256,640]{1,2,0:T(8,128)(2,1)S(1)}, u32[]{:S(2)}, u32[]{:S(2)}) %collective-permute-start.3) | collective-permute-done | bytes 655392 | tf_op jit(solution)/shard_map/ppermute | solution.py:20
  122.6 2.1 collective-permute-done.8
  126.6 2.2 convolution_convert_fusion
  130.7 8.1 %all-to-all-start = ((bf16[256,8,640]{2,0,1:T(8,128)(2,1)}), bf16[256,8,640]{2,0,1:T(8,128)(2,1)}, u32[]{:S(2)}, u32[]{:S(2)}) async-start(bf16[256,8,640]{2,0,1:T(8,128)(2,1)} %bitcast.594), calls=%async_computation | async-start | bytes 5242880 | tf_op jit(solution)/shard_map/all_to_all | solution.py:104
  138.8 6.6 %convolution_convert_fusion.1 = bf16[256,640]{1,0:T(8,128)(2,1)} fusion(bf16[256,5120]{1,0:T(8,128)(2,1)} %all-gather.2.cloned.1.call-done, bf16[640,5120]{1,0:T(8,128)(2,1)} %param.10), kind=kOutput, calls=%fused_computation.275 | convolution fusion | flops 1677885440 | bytes 9502720 | tf_op jit(solution)/shard_map/dot_general | solution.py:55
  151.0 20.2 %all-to-all-done = bf16[256,8,640]{2,0,1:T(8,128)(2,1)} async-done(((bf16[256,8,640]{2,0,1:T(8,128)(2,1)}), bf16[256,8,640]{2,0,1:T(8,128)(2,1)}, u32[]{:S(2)}, u32[]{:S(2)}) %all-to-all-start) | async-done | bytes 2621472 | tf_op jit(solution)/shard_map/all_to_all | solution.py:104
  171.2 2.9 reduce_sum.101
  178.3 2.2 copy.264
  180.5 3.5 %fusion.217 = bf16[5,128,256]{2,1,0:T(8,128)(2,1)} fusion(bf16[512,5,128]{0,2,1:T(8,128)(2,1)} %bitcast.674, f32[5,256,512]{2,1,0:T(8,128)} %copy-done.7, f32[512,5]{0,1:T(8,128)S(1)} %get-tuple-element.50, pred[512,256]{0,1:T(8,128)(4,1)} %bitcast.657), kind=kOutput, calls=%fused_computation.268 | convolution fusion | flops 170557440 | bytes 3745792 | tf_op jit(solution)/shard_map/qhk,qhd->khd/dot_general | solution.py:131
  185.8 2.1 fusion.13
  252.8 2.4 pad_maximum_fusion.8
  257.2 5.1 %collective-permute-start.15 = (bf16[2,256,640]{2,1,0:T(8,128)(2,1)}, bf16[2,256,640]{2,1,0:T(8,128)(2,1)}, u32[]{:S(2)}, u32[]{:S(2)}) collective-permute-start(bf16[2,256,640]{2,1,0:T(8,128)(2,1)} %pad_maximum_fusion.7), channel_id=1, source_target_pairs={{0,64},{16,80},{32,96},{48,112},{64,0},{80,16},{96,32},{112,48},{1... | collective-permute-start | bytes 1966088 | tf_op jit(solution)/shard_map/ppermute | solution.py:20
  264.4 2.0 pad_maximum_fusion.4
  271.3 39.0 %collective-permute-done.17 = bf16[2,256,640]{2,1,0:T(8,128)(2,1)S(1)} collective-permute-done((bf16[2,256,640]{2,1,0:T(8,128)(2,1)S(1)}, bf16[2,256,640]{2,1,0:T(8,128)(2,1)S(1)}, u32[]{:S(2)}, u32[]{:S(2)}) %collective-permute-start.17) | collective-permute-done | bytes 655392 | tf_op jit(solution)/shard_map/ppermute | solution.py:20
  310.3 2.8 collective-permute-start.12
  314.3 2.2 copy.290
  316.5 2.6 fusion.214
  321.7 5.6 %collective-permute-done.12 = bf16[2,256,640]{2,1,0:T(8,128)(2,1)} collective-permute-done((bf16[2,256,640]{2,1,0:T(8,128)(2,1)}, bf16[2,256,640]{2,1,0:T(8,128)(2,1)}, u32[]{:S(2)}, u32[]{:S(2)}) %collective-permute-start.12) | collective-permute-done | bytes 655392 | tf_op jit(solution)/shard_map/ppermute | solution.py:20
  327.3 2.9 add_convert_fusion
  (353 shorter events, 130.9 us)
Async XLA Ops:
  7.2 131.6 %all-gather.2.cloned.1.call-start = ((), (), s32[]{:S(2)}) async-start(), calls=%async_computation.1 | async-start | bytes 2949120 | tf_op jit(solution)/shard_map/all_gather | solution.py:54
  9.8 97.4 %collective-permute-start.7 = (bf16[2,256,640]{1,2,0:T(8,128)(2,1)S(1)}, bf16[2,256,640]{1,2,0:T(8,128)(2,1)S(1)}, u32[]{:S(2)}, u32[]{:S(2)}) collective-permute-start(bf16[2,256,640]{1,2,0:T(8,128)(2,1)S(1)} %pad_maximum_fusion.2), channel_id=1, source_target_pairs={{0,112},{16,0},{32,16},{48,32},{64,48},{80,64},{96,80},{112,96},{1... | collective-permute-start | bytes 1966088 | tf_op jit(solution)/shard_map/ppermute | solution.py:20
  13.9 31.8 %collective-permute-start.6 = (bf16[2,256,640]{1,2,0:T(8,128)(2,1)S(1)}, bf16[2,256,640]{1,2,0:T(8,128)(2,1)}, u32[]{:S(2)}, u32[]{:S(2)}) collective-permute-start(bf16[2,256,640]{1,2,0:T(8,128)(2,1)S(1)} %pad_maximum_fusion.2), channel_id=1, source_target_pairs={{0,96},{16,112},{32,0},{48,16},{64,32},{80,48},{96,64},{112,80},{1... | collective-permute-start | bytes 1966088 | tf_op jit(solution)/shard_map/ppermute | solution.py:20
  14.7 89.3 %collective-permute-start.5 = (bf16[2,256,640]{1,2,0:T(8,128)(2,1)S(1)}, bf16[2,256,640]{1,2,0:T(8,128)(2,1)}, u32[]{:S(2)}, u32[]{:S(2)}) collective-permute-start(bf16[2,256,640]{1,2,0:T(8,128)(2,1)S(1)} %pad_maximum_fusion.2), channel_id=1, source_target_pairs={{0,80},{16,96},{32,112},{48,0},{64,16},{80,32},{96,48},{112,64},{1... | collective-permute-start | bytes 1966088 | tf_op jit(solution)/shard_map/ppermute | solution.py:20
  15.1 56.9 %collective-permute-start.4 = (bf16[2,256,640]{1,2,0:T(8,128)(2,1)S(1)}, bf16[2,256,640]{1,2,0:T(8,128)(2,1)}, u32[]{:S(2)}, u32[]{:S(2)}) collective-permute-start(bf16[2,256,640]{1,2,0:T(8,128)(2,1)S(1)} %pad_maximum_fusion.2), channel_id=1, source_target_pairs={{0,64},{16,80},{32,96},{48,112},{64,0},{80,16},{96,32},{112,48},{1... | collective-permute-start | bytes 1966088 | tf_op jit(solution)/shard_map/ppermute | solution.py:20
  18.0 6.5 %collective-permute-start = (bf16[256,640]{1,0:T(8,128)(2,1)S(1)}, bf16[256,640]{1,0:T(8,128)(2,1)S(1)}, u32[]{:S(2)}, u32[]{:S(2)}) collective-permute-start(bf16[256,640]{1,0:T(8,128)(2,1)S(1)} %copy-done.74), channel_id=1, source_target_pairs={{0,8},{8,0},{1,9},{9,1},{2,10},{10,2},{3,11},{11,3},{4,12},{12,4},... | collective-permute-start | bytes 983048 | tf_op jit(solution)/shard_map/ppermute | solution.py:16
  24.5 49.6 %collective-permute-start.2 = (bf16[2,256,640]{1,2,0:T(8,128)(2,1)S(1)}, bf16[2,256,640]{1,2,0:T(8,128)(2,1)}, u32[]{:S(2)}, u32[]{:S(2)}) collective-permute-start(bf16[2,256,640]{1,2,0:T(8,128)(2,1)S(1)} %pad_maximum_fusion.2), channel_id=1, source_target_pairs={{0,32},{16,48},{32,64},{48,80},{64,96},{80,112},{96,0},{112,16},{1... | collective-permute-start | bytes 1966088 | tf_op jit(solution)/shard_map/ppermute | solution.py:20
  25.7 88.5 %copy-start = (f32[5,512,256]{1,2,0:T(8,128)}, f32[5,512,256]{1,2,0:T(8,128)S(1)}, u32[]{:S(2)}) copy-start(f32[5,512,256]{1,2,0:T(8,128)S(1)} %get-tuple-element.71) | copy-start | bytes 7864324
  45.7 44.9 %collective-permute-start.1 = (bf16[2,256,640]{1,2,0:T(8,128)(2,1)S(1)}, bf16[2,256,640]{1,2,0:T(8,128)(2,1)S(1)}, u32[]{:S(2)}, u32[]{:S(2)}) collective-permute-start(bf16[2,256,640]{1,2,0:T(8,128)(2,1)S(1)} %pad_maximum_fusion.2), channel_id=1, source_target_pairs={{0,16},{16,32},{32,48},{48,64},{64,80},{80,96},{96,112},{112,0},{1... | collective-permute-start | bytes 1966088 | tf_op jit(solution)/shard_map/ppermute | solution.py:20
  72.0 48.3 %copy-start.62 = (bf16[1,256,640]{1,2,0:T(8,128)(2,1)}, bf16[1,256,640]{1,2,0:T(8,128)(2,1)S(1)}, u32[]{:S(2)}) copy-start(bf16[1,256,640]{1,2,0:T(8,128)(2,1)S(1)} %get-tuple-element.36) | copy-start | bytes 983044
  72.0 30.4 %collective-permute-start.3 = (bf16[2,256,640]{1,2,0:T(8,128)(2,1)S(1)}, bf16[2,256,640]{1,2,0:T(8,128)(2,1)S(1)}, u32[]{:S(2)}, u32[]{:S(2)}) collective-permute-start(bf16[2,256,640]{1,2,0:T(8,128)(2,1)S(1)} %pad_maximum_fusion.2), channel_id=1, source_target_pairs={{0,48},{16,64},{32,80},{48,96},{64,112},{80,0},{96,16},{112,32},{1... | collective-permute-start | bytes 1966088 | tf_op jit(solution)/shard_map/ppermute | solution.py:20
  122.6 2.2 collective-permute-start.8
  130.7 40.5 %all-to-all-start = ((bf16[256,8,640]{2,0,1:T(8,128)(2,1)}), bf16[256,8,640]{2,0,1:T(8,128)(2,1)}, u32[]{:S(2)}, u32[]{:S(2)}) async-start(bf16[256,8,640]{2,0,1:T(8,128)(2,1)} %bitcast.594), calls=%async_computation | async-start | bytes 5242880 | tf_op jit(solution)/shard_map/all_to_all | solution.py:104
  151.0 23.6 %collective-permute-start.9 = (f32[256,10]{0,1:T(8,128)}, f32[256,10]{0,1:T(8,128)}, u32[]{:S(2)}, u32[]{:S(2)}) collective-permute-start(f32[256,10]{0,1:T(8,128)} %pad_maximum_fusion.12), channel_id=1, source_target_pairs={{0,8},{8,0},{1,9},{9,1},{2,10},{10,2},{3,11},{11,3},{4,12},{12,4},... | collective-permute-start | bytes 30728 | tf_op jit(solution)/shard_map/ppermute | solution.py:16
  174.1 2.2 collective-permute-start.10
  249.2 21.6 %collective-permute-start.18 = (bf16[2,256,640]{2,1,0:T(8,128)(2,1)S(1)}, bf16[2,256,640]{2,1,0:T(8,128)(2,1)S(1)}, u32[]{:S(2)}, u32[]{:S(2)}) collective-permute-start(bf16[2,256,640]{2,1,0:T(8,128)(2,1)S(1)} %pad_maximum_fusion.10), channel_id=1, source_target_pairs={{0,16},{16,32},{32,48},{48,64},{64,80},{80,96},{96,112},{112,0},{1... | collective-permute-start | bytes 1966088 | tf_op jit(solution)/shard_map/ppermute | solution.py:20
  251.8 58.6 %collective-permute-start.17 = (bf16[2,256,640]{2,1,0:T(8,128)(2,1)S(1)}, bf16[2,256,640]{2,1,0:T(8,128)(2,1)S(1)}, u32[]{:S(2)}, u32[]{:S(2)}) collective-permute-start(bf16[2,256,640]{2,1,0:T(8,128)(2,1)S(1)} %pad_maximum_fusion.9), channel_id=1, source_target_pairs={{0,32},{16,48},{32,64},{48,80},{64,96},{80,112},{96,0},{112,16},{1... | collective-permute-start | bytes 1966088 | tf_op jit(solution)/shard_map/ppermute | solution.py:20
  255.3 63.9 %collective-permute-start.16 = (bf16[2,256,640]{2,1,0:T(8,128)(2,1)}, bf16[2,256,640]{2,1,0:T(8,128)(2,1)}, u32[]{:S(2)}, u32[]{:S(2)}) collective-permute-start(bf16[2,256,640]{2,1,0:T(8,128)(2,1)} %pad_maximum_fusion.8), channel_id=1, source_target_pairs={{0,48},{16,64},{32,80},{48,96},{64,112},{80,0},{96,16},{112,32},{1... | collective-permute-start | bytes 1966088 | tf_op jit(solution)/shard_map/ppermute | solution.py:20
  257.2 64.1 %collective-permute-start.15 = (bf16[2,256,640]{2,1,0:T(8,128)(2,1)}, bf16[2,256,640]{2,1,0:T(8,128)(2,1)}, u32[]{:S(2)}, u32[]{:S(2)}) collective-permute-start(bf16[2,256,640]{2,1,0:T(8,128)(2,1)} %pad_maximum_fusion.7), channel_id=1, source_target_pairs={{0,64},{16,80},{32,96},{48,112},{64,0},{80,16},{96,32},{112,48},{1... | collective-permute-start | bytes 1966088 | tf_op jit(solution)/shard_map/ppermute | solution.py:20
  264.4 57.0 %collective-permute-start.14 = (bf16[2,256,640]{2,1,0:T(8,128)(2,1)}, bf16[2,256,640]{2,1,0:T(8,128)(2,1)}, u32[]{:S(2)}, u32[]{:S(2)}) collective-permute-start(bf16[2,256,640]{2,1,0:T(8,128)(2,1)} %pad_maximum_fusion.6), channel_id=1, source_target_pairs={{0,80},{16,96},{32,112},{48,0},{64,16},{80,32},{96,48},{112,64},{1... | collective-permute-start | bytes 1966088 | tf_op jit(solution)/shard_map/ppermute | solution.py:20
  268.2 48.3 %copy-start.2 = (f32[5,512,256]{1,2,0:T(8,128)S(1)}, f32[5,512,256]{1,2,0:T(8,128)}, u32[]{:S(2)}) copy-start(f32[5,512,256]{1,2,0:T(8,128)} %copy-done) | copy-start | bytes 7864324
  270.9 50.9 %collective-permute-start.13 = (bf16[2,256,640]{2,1,0:T(8,128)(2,1)}, bf16[2,256,640]{2,1,0:T(8,128)(2,1)}, u32[]{:S(2)}, u32[]{:S(2)}) collective-permute-start(bf16[2,256,640]{2,1,0:T(8,128)(2,1)} %pad_maximum_fusion.5), channel_id=1, source_target_pairs={{0,96},{16,112},{32,0},{48,16},{64,32},{80,48},{96,64},{112,80},{1... | collective-permute-start | bytes 1966088 | tf_op jit(solution)/shard_map/ppermute | solution.py:20
  310.3 17.0 %collective-permute-start.12 = (bf16[2,256,640]{2,1,0:T(8,128)(2,1)}, bf16[2,256,640]{2,1,0:T(8,128)(2,1)}, u32[]{:S(2)}, u32[]{:S(2)}) collective-permute-start(bf16[2,256,640]{2,1,0:T(8,128)(2,1)} %pad_maximum_fusion.4), channel_id=1, source_target_pairs={{0,112},{16,0},{32,16},{48,32},{64,48},{80,64},{96,80},{112,96},{1... | collective-permute-start | bytes 1966088 | tf_op jit(solution)/shard_map/ppermute | solution.py:20
  319.2 12.0 %collective-permute-start.11 = (f32[256,640]{1,0:T(8,128)}, f32[256,640]{1,0:T(8,128)S(1)}, u32[]{:S(2)}, u32[]{:S(2)}) collective-permute-start(f32[256,640]{1,0:T(8,128)} %copy.290), channel_id=1, source_target_pairs={{0,8},{8,0},{1,9},{9,1},{2,10},{10,2},{3,11},{11,3},{4,12},{12,4},... | collective-permute-start | bytes 1966088 | tf_op jit(solution)/shard_map/ppermute | solution.py:16
  (81 other events, 830.0 us)
Sparse Core Ops, SparseCore 0:
  18.1 61.8 all-gather.1
